TPU v7x, 512 devices: a whole 4x4x16 slice. The times are simulated.
512 devices in a mesh: fibre: 32 (over z, core), group: 16 (over y, x).
Axes of the slice: x: 4, y: 4, z: 16, core: 2. Of those that a mesh axis runs over, the one named last changes fastest.
Arguments:
- species_field: float32 [512, 524288], P('fibre', 'group'), may hold values from -45 to 45, as said below
- start_block: float32 [512, 64], replicated, may hold values from -4 to 4
Outputs:
- mode_basis: float32 [512, 64], replicated
- core_tensor: float32 [64, 524288], P(None, ('group', 'fibre'))
Inputs may be any that keep to these rules, and one draw needn't show every extreme that they name: `species_field`: float32 field values.
All inputs are finite; a program needn't handle non-finite values.
Results may differ from a plain program's by a relative error of at most 0.0003.
Values sent between devices are 32-bit elements; how exact they have to be, the bound alone decides.
No kernel may reach another device: no remote copies, remote signals or barrier semaphores. Data moves between devices by JAX's collectives and lax.ppermute only.
A program may use at most 64 MiB of HBM per device.

v0:
```python
import jax
import jax.numpy as jnp
from jax import lax
from jax.sharding import PartitionSpec as P

ITERS = 3


highest_precision = lax.Precision.HIGHEST


def orthonormal(matrix):
    inner_gram = jnp.dot(matrix.T, matrix, precision=highest_precision)
    lower_factor = jnp.linalg.cholesky(inner_gram)
    return lax.linalg.triangular_solve(
        lower_factor, matrix, left_side=False, lower=True, transpose_a=True
    )


def on_device(species_field, start_block):
    fibres = lax.all_to_all(species_field, "fibre", split_axis=1, concat_axis=0, tiled=True)
    total_columns = fibres.shape[1] * lax.axis_size("fibre") * lax.axis_size("group")
    mode_basis = orthonormal(start_block)
    local_gram = jnp.dot(fibres, fibres.T, precision=highest_precision) / total_columns
    gram_matrix = lax.psum(local_gram, ("fibre", "group"))
    for iteration in range(ITERS):
        mode_basis = orthonormal(jnp.dot(gram_matrix, mode_basis, precision=highest_precision))
    core_tensor = jnp.dot(mode_basis.T, fibres, precision=highest_precision)
    return (mode_basis, core_tensor)


def solution(mesh):
    placed = (P("fibre", "group"), P())
    return jax.shard_map(
        on_device,
        mesh=mesh,
        in_specs=placed,
        out_specs=(P(), P(None, ("group", "fibre"))),
        check_vma=False,
    )
```

profile of v0, /device:TPU:1, one launch (start us, length us, event | category | flops | bytes accessed | tf_op | source)
XLA Modules:
  0.0 643.5 jit_solution(7276870236529994059)
XLA Ops:
  7.2 0.0 copy-start
  7.2 3.2 copy.24
  10.4 16.7 %all-to-all-start = ((f32[16,32,1024]{2,0,1:T(8,128)}), f32[16,32,1024]{2,0,1:T(8,128)S(1)}, u32[]{:S(2)}, u32[]{:S(2)}) async-start(f32[16,32,1024]{2,0,1:T(8,128)} %bitcast.75), calls=%async_computation | async-start | bytes 4194304 | tf_op jit(solution)/shard_map/all_to_all | solution.py:21
  27.2 0.0 all-reduce.2.cloned.1.call-start
  27.2 0.0 copy-done
  27.2 0.3 fusion.18
  27.5 0.1 copy.18
  27.6 5.8 cholesky.74
  33.5 92.3 %all-to-all-done = f32[16,32,1024]{2,0,1:T(8,128)S(1)} async-done(((f32[16,32,1024]{2,0,1:T(8,128)}), f32[16,32,1024]{2,0,1:T(8,128)S(1)}, u32[]{:S(2)}, u32[]{:S(2)}) %all-to-all-start) | async-done | bytes 2097184 | tf_op jit(solution)/shard_map/all_to_all | solution.py:21
  125.8 4.6 convolution_multiply_fusion
  130.3 0.0 all-reduce.2.cloned.1.call-update
  130.4 0.6 compare_reduce_fusion.3
  131.0 0.7 fusion
  131.6 4.9 custom-call.8
  136.5 0.3 convolution_bitcast_fusion.3
  136.9 454.4 %all-reduce.2.cloned.1.call-done = f32[512,512]{1,0:T(8,128)} async-done(((f32[512,512]{1,0:T(8,128)}), f32[512,512]{1,0:T(8,128)}) %all-reduce.2.cloned.1.call-update) | async-done | bytes 1048592 | tf_op jit(solution)/shard_map/psum | solution.py:25
  591.3 0.0 copy-start.1
  591.3 2.4 fusion.19
  593.7 0.3 fusion.20
  594.0 0.1 copy.19
  594.1 5.8 cholesky.85
  600.0 0.6 compare_reduce_fusion.2
  600.6 0.7 fusion.1
  601.3 4.9 custom-call.9
  606.2 0.3 convolution_bitcast_fusion.2
  606.5 0.0 copy-done.1
  606.5 1.1 fusion.21
  607.6 0.3 fusion.22
  607.9 0.1 copy.20
  608.0 5.8 cholesky.96
  613.9 0.6 compare_reduce_fusion.1
  614.5 0.7 fusion.2
  615.2 4.9 custom-call.10
  620.1 0.3 convolution_bitcast_fusion.1
  620.4 1.3 fusion.23
  621.8 0.3 fusion.24
  622.0 0.1 copy.21
  622.1 5.8 cholesky.107
  628.0 0.6 compare_reduce_fusion
  628.6 0.7 fusion.3
  629.3 4.9 custom-call.11
  634.2 0.3 convolution_bitcast_fusion
  634.5 0.0 copy-start.2
  634.6 2.1 fusion.25
  636.6 0.0 copy-done.2
  (8 shorter events, 0.2 us)
Async XLA Ops:
  7.2 20.0 %copy-start = (f32[512,64]{0,1:T(8,128)S(1)}, f32[512,64]{0,1:T(8,128)}, u32[]{:S(2)}) copy-start(f32[512,64]{0,1:T(8,128)} %param.6) | copy-start | bytes 393220
  10.4 115.4 %all-to-all-start = ((f32[16,32,1024]{2,0,1:T(8,128)}), f32[16,32,1024]{2,0,1:T(8,128)S(1)}, u32[]{:S(2)}, u32[]{:S(2)}) async-start(f32[16,32,1024]{2,0,1:T(8,128)} %bitcast.75), calls=%async_computation | async-start | bytes 4194304 | tf_op jit(solution)/shard_map/all_to_all | solution.py:21
  27.2 564.1 %all-reduce.2.cloned.1.call-start = ((), (), s32[]{:S(2)}) async-start(), calls=%async_computation.1 | async-start | bytes 2097152 | tf_op jit(solution)/shard_map/psum | solution.py:25
  591.3 15.2 %copy-start.1 = (f32[512,512]{1,0:T(8,128)S(1)}, f32[512,512]{1,0:T(8,128)}, u32[]{:S(2)}) copy-start(f32[512,512]{1,0:T(8,128)} %all-reduce.2.cloned.1.call-done) | copy-start | bytes 3145732
  634.5 2.1 copy-start.2
Sparse Core Ops, SparseCore 0:
  130.5 460.7 all-reduce.1
where the time goes:
time: 644 us; the launch traced here: 643 us
  waiting for transfers between devices  547 us (85%)
  other arithmetic  48.3 us (8%)
  starting transfers between devices  16.8 us (3%)
  between operations  14.2 us (2%)
  matrix products  13.9 us (2%)
    psum x1, waiting for transfers between devices, on_device(): gram_matrix = lax.psum(local_gram, ('fibre', 'group'))  454 us
    all_to_all x1, waiting for transfers between devices, on_device(): lax.all_to_all(species_field, 'fibre', split_axis=1, concat_axis=0, tiled...  92.3 us
    another operation x12, other arithmetic, orthonormal(): lower_factor = jnp.linalg.cholesky(inner_gram)  26.1 us
    another operation x8, other arithmetic, orthonormal(): lax.linalg.triangular_solve(lower_factor, matrix, left_side=False, lower=...  22.2 us
    all_to_all x1, starting transfers between devices, on_device(): lax.all_to_all(species_field, 'fibre', split_axis=1, concat_axis=0, tiled...  16.7 us
  transfers between devices with their start and end apart: 2, of which 2 were waited for; matrix products, arithmetic and copies ran while one was open for 2% of the time, Pallas kernels for 0%

commit v1 on v0

--- a/solution.py
+++ b/solution.py
@@ -17,12 +17,35 @@
     )
 
 
+def exchange(blocks, axis):
+    return lax.all_to_all(blocks, axis, 0, 0, tiled=True)
+
+
+def reduce_scatter(matrix, axis):
+    parts = lax.axis_size(axis)
+    blocks = matrix.reshape(parts, matrix.shape[0] // parts, *matrix.shape[1:])
+    return exchange(blocks, axis).sum(0)
+
+
+def gather(matrix, axis):
+    parts = lax.axis_size(axis)
+    blocks = jnp.broadcast_to(matrix[None], (parts,) + matrix.shape)
+    return exchange(blocks, axis).reshape(parts * matrix.shape[0], *matrix.shape[1:])
+
+
+def all_reduce(matrix):
+    rows = reduce_scatter(matrix, "group")
+    rows = reduce_scatter(rows, "fibre")
+    rows = gather(rows, "fibre")
+    return gather(rows, "group")
+
+
 def on_device(species_field, start_block):
     fibres = lax.all_to_all(species_field, "fibre", split_axis=1, concat_axis=0, tiled=True)
     total_columns = fibres.shape[1] * lax.axis_size("fibre") * lax.axis_size("group")
     mode_basis = orthonormal(start_block)
     local_gram = jnp.dot(fibres, fibres.T, precision=highest_precision) / total_columns
-    gram_matrix = lax.psum(local_gram, ("fibre", "group"))
+    gram_matrix = all_reduce(local_gram)
     for iteration in range(ITERS):
         mode_basis = orthonormal(jnp.dot(gram_matrix, mode_basis, precision=highest_precision))
     core_tensor = jnp.dot(mode_basis.T, fibres, precision=highest_precision)

time: 644 us -> 246 us (0.38)
  waiting for transfers between devices: 547 us -> 2.3 us
  blocking collectives: 0 us -> 175 us
  between operations: 14.2 us -> 0.85 us
  starting transfers between devices: 16.8 us -> 3.83 us
    psum x1 -> x0, waiting for transfers between devices: 454 us -> none  [on_device(): gram_matrix = lax.psum(local_gram, ('fibre', 'group'))]
    all_to_all x0 -> x4, blocking collectives: none -> 175 us  [the longest x1 117 us: on_device(): lax.all_to_all(species_field, 'fibre', split_axis=1, concat_axis=0, tiled...]
    all_to_all x1, waiting for transfers between devices: 92.3 us -> 2.3 us  [exchange(): return lax.all_to_all(blocks, axis, 0, 0, tiled=True)]
    all_to_all x1, starting transfers between devices: 16.7 us -> 3.83 us  [exchange(): return lax.all_to_all(blocks, axis, 0, 0, tiled=True)]
  transfers between devices with their start and end apart: 2 -> 1, of which waited for: 2 -> 1; matrix products, arithmetic and copies ran while one was open for 2% -> 5% of each run, Pallas kernels for 0% -> 0%
where the time goes in v1:
time: 246 us; the launch traced here: 245 us
  blocking collectives  175 us (71%)
  other arithmetic  48.5 us (20%)
  matrix products  11.4 us (5%)
  starting transfers between devices  3.83 us (2%)
  local copies, waits for them, and re-layouts  3.28 us (1%)
    all_to_all x1, blocking collectives, on_device(): lax.all_to_all(species_field, 'fibre', split_axis=1, concat_axis=0, tiled...  117 us
    all_to_all x3, blocking collectives, exchange(): return lax.all_to_all(blocks, axis, 0, 0, tiled=True)  57.7 us
    another operation x12, other arithmetic, orthonormal(): lower_factor = jnp.linalg.cholesky(inner_gram)  26.1 us
    another operation x8, other arithmetic, orthonormal(): lax.linalg.triangular_solve(lower_factor, matrix, left_side=False, lower=...  22.2 us
  transfers between devices with their start and end apart: 1, of which 1 were waited for; matrix products, arithmetic and copies ran while one was open for 5% of the time, Pallas kernels for 0%

profile of v1, /device:TPU:1, one launch (start us, length us, event | category | flops | bytes accessed | tf_op | source)
XLA Modules:
  0.0 245.0 jit_solution(12905478632010260943)
XLA Ops:
  0.6 0.0 copy-start
  0.6 1.8 copy.26
  2.4 117.2 %all_to_all.39 = f32[16,32,1024]{2,0,1:T(8,128)S(1)} all-to-all(f32[16,32,1024]{2,0,1:T(8,128)S(1)} %bitcast.83), channel_id=1, replica_groups=mesh['fibre'=32,'group'=16] {'fibre'}, dimensions={1} | all-to-all | bytes 4194304 | tf_op jit(solution)/shard_map/all_to_all | solution.py:44
  119.6 3.5 %convolution_multiply_fusion = f32[512,512]{1,0:T(8,128)S(1)} fusion(f32[512,1024]{1,0:T(8,128)S(1)} %bitcast.78), kind=kOutput, calls=%fused_computation.1 | convolution fusion | flops 3221487616 | bytes 3145728 | tf_op jit(solution)/shard_map/dot_general | solution.py:47
  123.2 22.7 %all_to_all.40 = f32[16,32,512]{2,1,0:T(8,128)S(1)} all-to-all(f32[16,32,512]{2,1,0:T(8,128)S(1)} %bitcast.84), channel_id=1, replica_groups=mesh['fibre'=32,'group'=16] {'group'}, dimensions={0} | all-to-all | bytes 2097152 | tf_op jit(solution)/shard_map/all_to_all | solution.py:21
  145.9 0.1 reduce_sum.18
  146.0 17.6 %all_to_all.41 = f32[32,1,512]{2,1,0:T(1,128)S(1)} all-to-all(f32[32,1,512]{2,1,0:T(1,128)S(1)} %reshape.34), channel_id=1, replica_groups=mesh['fibre'=32,'group'=16] {'fibre'}, dimensions={0} | all-to-all | bytes 131072 | tf_op jit(solution)/shard_map/all_to_all | solution.py:21
  163.6 0.1 reduce_sum.19
  163.7 17.3 %all_to_all.42 = f32[32,1,512]{2,1,0:T(1,128)S(1)} all-to-all(f32[32,1,512]{2,1,0:T(1,128)S(1)} %broadcast_in_dim.7), channel_id=1, replica_groups=mesh['fibre'=32,'group'=16] {'fibre'}, dimensions={0} | all-to-all | bytes 131072 | tf_op jit(solution)/shard_map/all_to_all | solution.py:21
  181.1 1.1 broadcast_in_dim.16
  182.2 3.8 %all-to-all-start.4 = ((f32[16,32,512]{2,1,0:T(8,128)}), f32[16,32,512]{2,1,0:T(8,128)S(1)}, u32[]{:S(2)}, u32[]{:S(2)}) async-start(f32[16,32,512]{2,1,0:T(8,128)} %broadcast_in_dim.16), calls=%async_computation.4 | async-start | bytes 2097152 | tf_op jit(solution)/shard_map/all_to_all | solution.py:21
  186.0 0.0 copy-done
  186.0 0.3 fusion.18
  186.3 0.1 copy.18
  186.4 5.8 %cholesky.74 = f32[64,64]{1,0:T(8,128)S(1)} custom-call(f32[64,64]{1,0:T(8,128)S(1)} %fusion.11), custom_call_target="Cholesky" | custom-call | tf_op jit(solution)/shard_map/jit(cholesky)/cholesky | solution.py:14
  192.3 0.6 compare_reduce_fusion.3
  192.9 0.7 fusion
  193.6 4.9 %custom-call.8 = f32[1,64,64]{1,2,0:T(8,128)S(1)} custom-call(f32[1,64,64]{2,1,0:T(8,128)S(1)} %fusion), custom_call_target="InvertDiagBlocksLowerTriangular" | custom-call | tf_op jit(solution)/shard_map/triangular_solve/custom-call.0 | solution.py:15
  198.5 0.3 convolution_bitcast_fusion.3
  198.8 2.3 all-to-all-done.4
  201.1 1.1 fusion.19
  202.3 0.3 fusion.20
  202.5 0.1 copy.19
  202.6 5.8 %cholesky.85 = f32[64,64]{1,0:T(8,128)S(1)} custom-call(f32[64,64]{1,0:T(8,128)S(1)} %fusion.9), custom_call_target="Cholesky" | custom-call | tf_op jit(solution)/shard_map/jit(cholesky)/cholesky | solution.py:14
  208.5 0.6 compare_reduce_fusion.2
  209.1 0.7 fusion.1
  209.8 4.9 %custom-call.9 = f32[1,64,64]{1,2,0:T(8,128)S(1)} custom-call(f32[1,64,64]{2,1,0:T(8,128)S(1)} %fusion.1), custom_call_target="InvertDiagBlocksLowerTriangular" | custom-call | tf_op jit(solution)/shard_map/triangular_solve/custom-call.0 | solution.py:15
  214.7 0.3 convolution_bitcast_fusion.2
  215.0 1.1 fusion.21
  216.2 0.3 fusion.22
  216.5 0.1 copy.20
  216.5 5.8 %cholesky.96 = f32[64,64]{1,0:T(8,128)S(1)} custom-call(f32[64,64]{1,0:T(8,128)S(1)} %fusion.7), custom_call_target="Cholesky" | custom-call | tf_op jit(solution)/shard_map/jit(cholesky)/cholesky | solution.py:14
  222.4 0.6 compare_reduce_fusion.1
  223.1 0.7 fusion.2
  223.7 4.9 %custom-call.10 = f32[1,64,64]{1,2,0:T(8,128)S(1)} custom-call(f32[1,64,64]{2,1,0:T(8,128)S(1)} %fusion.2), custom_call_target="InvertDiagBlocksLowerTriangular" | custom-call | tf_op jit(solution)/shard_map/triangular_solve/custom-call.0 | solution.py:15
  228.6 0.3 convolution_bitcast_fusion.1
  229.0 1.1 fusion.23
  230.1 0.3 fusion.24
  230.4 0.1 copy.21
  230.5 5.8 %cholesky.107 = f32[64,64]{1,0:T(8,128)S(1)} custom-call(f32[64,64]{1,0:T(8,128)S(1)} %fusion.5), custom_call_target="Cholesky" | custom-call | tf_op jit(solution)/shard_map/jit(cholesky)/cholesky | solution.py:14
  236.4 0.6 compare_reduce_fusion
  237.0 0.7 fusion.3
  237.7 4.9 %custom-call.11 = f32[1,64,64]{1,2,0:T(8,128)S(1)} custom-call(f32[1,64,64]{2,1,0:T(8,128)S(1)} %fusion.3), custom_call_target="InvertDiagBlocksLowerTriangular" | custom-call | tf_op jit(solution)/shard_map/triangular_solve/custom-call.0 | solution.py:15
  242.6 0.3 convolution_bitcast_fusion
  242.9 0.0 copy-start.1
  242.9 2.1 fusion.25
  245.0 0.0 copy-done.1
  (11 shorter events, 0.2 us)
Async XLA Ops:
  0.6 185.4 %copy-start = (f32[512,64]{0,1:T(8,128)S(1)}, f32[512,64]{0,1:T(8,128)}, u32[]{:S(2)}) copy-start(f32[512,64]{0,1:T(8,128)} %param.6) | copy-start | bytes 393220
  182.2 18.9 %all-to-all-start.4 = ((f32[16,32,512]{2,1,0:T(8,128)}), f32[16,32,512]{2,1,0:T(8,128)S(1)}, u32[]{:S(2)}, u32[]{:S(2)}) async-start(f32[16,32,512]{2,1,0:T(8,128)} %broadcast_in_dim.16), calls=%async_computation.4 | async-start | bytes 2097152 | tf_op jit(solution)/shard_map/all_to_all | solution.py:21
  242.9 2.1 copy-start.1

commit v2 on v1

--- a/solution.py
+++ b/solution.py
@@ -1,6 +1,7 @@
 import jax
 import jax.numpy as jnp
 from jax import lax
+from jax.experimental import pallas as pl
 from jax.sharding import PartitionSpec as P
 
 ITERS = 3
@@ -9,11 +10,34 @@
 highest_precision = lax.Precision.HIGHEST
 
 
+def inverse_cholesky_kernel(inner_ref, inverse_ref):
+    size = inner_ref.shape[0]
+    schur = inner_ref[...]
+    rows = lax.broadcasted_iota(jnp.int32, (size, 1), 0)
+    cols = lax.broadcasted_iota(jnp.int32, (1, size), 1)
+    inverse = (rows == cols).astype(jnp.float32)
+    for j in range(size):
+        inv_pivot = lax.rsqrt(schur[j:j + 1, j:j + 1])
+        factor_col = jnp.where(rows >= j, schur[:, j:j + 1] * inv_pivot, 0.0)
+        factor_row = jnp.where(cols >= j, schur[j:j + 1, :] * inv_pivot, 0.0)
+        schur = schur - factor_col * factor_row
+        step = jnp.where(rows > j, factor_col * inv_pivot, jnp.where(rows == j, 1.0 - inv_pivot, 0.0))
+        inverse = inverse - step * inverse[j:j + 1, :]
+    inverse_ref[...] = inverse
+
+
+def inverse_cholesky(inner_gram):
+    return pl.pallas_call(
+        inverse_cholesky_kernel,
+        out_shape=jax.ShapeDtypeStruct(inner_gram.shape, jnp.float32),
+    )(inner_gram)
+
+
 def orthonormal(matrix):
     inner_gram = jnp.dot(matrix.T, matrix, precision=highest_precision)
-    lower_factor = jnp.linalg.cholesky(inner_gram)
-    return lax.linalg.triangular_solve(
-        lower_factor, matrix, left_side=False, lower=True, transpose_a=True
+    lower_inverse = inverse_cholesky(inner_gram)
+    return lax.dot_general(
+        matrix, lower_inverse, (((1,), (1,)), ((), ())), precision=highest_precision
     )
 
 

time: 246 us -> 234 us (0.951)
  other arithmetic: 48.5 us -> 0.14 us
  Pallas kernels: 0 us -> 26.6 us
  matrix products: 11.4 us -> 16.6 us
  waiting for transfers between devices: 2.3 us -> 6.53 us
    another operation x20 -> x0, other arithmetic: 48.3 us -> none  [the longest x12 26.1 us: orthonormal(): lower_factor = jnp.linalg.cholesky(inner_gram)]
    pallas_call x0 -> x4, Pallas kernels: none -> 26.6 us  [inverse_cholesky(): pl.pallas_call(inverse_cholesky_kernel, out_shape=jax.ShapeDtypeStruct(in...]
    all_to_all x1, waiting for transfers between devices: 2.3 us -> 6.53 us  [exchange(): return lax.all_to_all(blocks, axis, 0, 0, tiled=True)]
    dot_general x0 -> x4, matrix products: none -> 4.07 us  [orthonormal(): lax.dot_general(matrix, lower_inverse, (((1,), (1,)), ((), ())), precisio...]
    dot_general x4, matrix products: 1.04 us -> 3.52 us  [orthonormal(): inner_gram = jnp.dot(matrix.T, matrix, precision=highest_precision)]
  transfers between devices with their start and end apart: 1 -> 1, of which waited for: 1 -> 1; matrix products, arithmetic and copies ran while one was open for 5% -> 1% of each run, Pallas kernels for 0% -> 3%
where the time goes in v2:
time: 234 us; the launch traced here: 232 us
  blocking collectives  175 us (75%)
  Pallas kernels  26.6 us (11%)
  matrix products  16.6 us (7%)
  waiting for transfers between devices  6.53 us (3%)
  starting transfers between devices  3.83 us (2%)
  local copies, waits for them, and re-layouts  2.99 us (1%)
    all_to_all x1, blocking collectives, on_device(): lax.all_to_all(species_field, 'fibre', split_axis=1, concat_axis=0, tiled...  117 us
    all_to_all x3, blocking collectives, exchange(): return lax.all_to_all(blocks, axis, 0, 0, tiled=True)  57.7 us
    pallas_call x4, Pallas kernels, inverse_cholesky(): pl.pallas_call(inverse_cholesky_kernel, out_shape=jax.ShapeDtypeStruct(in...  26.6 us
    all_to_all x1, waiting for transfers between devices, exchange(): return lax.all_to_all(blocks, axis, 0, 0, tiled=True)  6.53 us
  transfers between devices with their start and end apart: 1, of which 1 were waited for; matrix products, arithmetic and copies ran while one was open for 1% of the time, Pallas kernels for 3%

profile of v2, /device:TPU:1, one launch (start us, length us, event | category | flops | bytes accessed | tf_op | source)
XLA Modules:
  0.0 232.3 jit_solution(12857614697216048314)
XLA Ops:
  0.6 0.0 copy-start
  0.6 1.8 copy.10
  2.4 117.2 %all_to_all.39 = f32[16,32,1024]{2,0,1:T(8,128)S(1)} all-to-all(f32[16,32,1024]{2,0,1:T(8,128)S(1)} %bitcast.43), channel_id=1, replica_groups=mesh['fibre'=32,'group'=16] {'fibre'}, dimensions={1} | all-to-all | bytes 4194304 | tf_op jit(solution)/shard_map/all_to_all | solution.py:68
  119.6 3.5 %convolution_multiply_fusion = f32[512,512]{1,0:T(8,128)S(1)} fusion(f32[512,1024]{1,0:T(8,128)S(1)} %bitcast.38), kind=kOutput, calls=%fused_computation.1 | convolution fusion | flops 3221487616 | bytes 3145728 | tf_op jit(solution)/shard_map/dot_general | solution.py:71
  123.2 22.7 %all_to_all.40 = f32[16,32,512]{2,1,0:T(8,128)S(1)} all-to-all(f32[16,32,512]{2,1,0:T(8,128)S(1)} %bitcast.44), channel_id=1, replica_groups=mesh['fibre'=32,'group'=16] {'group'}, dimensions={0} | all-to-all | bytes 2097152 | tf_op jit(solution)/shard_map/all_to_all | solution.py:45
  145.9 0.1 reduce_sum.18
  146.0 17.6 %all_to_all.41 = f32[32,1,512]{2,1,0:T(1,128)S(1)} all-to-all(f32[32,1,512]{2,1,0:T(1,128)S(1)} %reshape.23), channel_id=1, replica_groups=mesh['fibre'=32,'group'=16] {'fibre'}, dimensions={0} | all-to-all | bytes 131072 | tf_op jit(solution)/shard_map/all_to_all | solution.py:45
  163.6 0.1 reduce_sum.19
  163.7 17.3 %all_to_all.42 = f32[32,1,512]{2,1,0:T(1,128)S(1)} all-to-all(f32[32,1,512]{2,1,0:T(1,128)S(1)} %broadcast_in_dim.6), channel_id=1, replica_groups=mesh['fibre'=32,'group'=16] {'fibre'}, dimensions={0} | all-to-all | bytes 131072 | tf_op jit(solution)/shard_map/all_to_all | solution.py:45
  181.1 1.1 broadcast_in_dim.15
  182.2 3.8 %all-to-all-start.4 = ((f32[16,32,512]{2,1,0:T(8,128)}), f32[16,32,512]{2,1,0:T(8,128)S(1)}, u32[]{:S(2)}, u32[]{:S(2)}) async-start(f32[16,32,512]{2,1,0:T(8,128)} %broadcast_in_dim.15), calls=%async_computation.4 | async-start | bytes 2097152 | tf_op jit(solution)/shard_map/all_to_all | solution.py:45
  186.0 0.0 copy-done
  186.0 0.9 fusion.inner_ref
  186.9 6.7 %shard_map.41 = f32[64,64]{1,0:T(8,128)} custom-call(f32[64,64]{1,0:T(8,128)} %fusion.inner_ref), custom_call_target="tpu_custom_call" | custom-call | tf_op jit(solution)/shard_map/pallas_call | solution.py:30
  193.6 1.0 fusion.1
  194.6 6.5 %all-to-all-done.4 = f32[16,32,512]{2,1,0:T(8,128)S(1)} async-done(((f32[16,32,512]{2,1,0:T(8,128)}), f32[16,32,512]{2,1,0:T(8,128)S(1)}, u32[]{:S(2)}, u32[]{:S(2)}) %all-to-all-start.4) | async-done | bytes 1048608 | tf_op jit(solution)/shard_map/all_to_all | solution.py:45
  201.1 1.1 fusion.2
  202.3 0.9 fusion.3.inner_ref
  203.1 6.7 %shard_map.42 = f32[64,64]{1,0:T(8,128)} custom-call(f32[64,64]{1,0:T(8,128)} %fusion.3.inner_ref), custom_call_target="tpu_custom_call" | custom-call | tf_op jit(solution)/shard_map/pallas_call | solution.py:30
  209.8 1.0 fusion.4
  210.8 1.1 fusion.5
  212.0 0.9 fusion.6.inner_ref
  212.8 6.7 %shard_map.43 = f32[64,64]{1,0:T(8,128)} custom-call(f32[64,64]{1,0:T(8,128)} %fusion.6.inner_ref), custom_call_target="tpu_custom_call" | custom-call | tf_op jit(solution)/shard_map/pallas_call | solution.py:30
  219.5 1.0 fusion.7
  220.5 1.1 fusion.8
  221.7 0.9 fusion.9.inner_ref
  222.6 6.7 %shard_map.44 = f32[64,64]{1,0:T(8,128)} custom-call(f32[64,64]{1,0:T(8,128)} %fusion.9.inner_ref), custom_call_target="tpu_custom_call" | custom-call | tf_op jit(solution)/shard_map/pallas_call | solution.py:30
  229.2 1.0 fusion.10
  230.2 0.0 copy-start.1
  230.3 2.1 fusion.11
  232.3 0.0 copy-done.1
  (3 shorter events, 0.1 us)
Async XLA Ops:
  0.6 185.4 %copy-start = (f32[512,64]{0,1:T(8,128)S(1)}, f32[512,64]{0,1:T(8,128)}, u32[]{:S(2)}) copy-start(f32[512,64]{0,1:T(8,128)} %param.3) | copy-start | bytes 393220
  182.2 18.9 %all-to-all-start.4 = ((f32[16,32,512]{2,1,0:T(8,128)}), f32[16,32,512]{2,1,0:T(8,128)S(1)}, u32[]{:S(2)}, u32[]{:S(2)}) async-start(f32[16,32,512]{2,1,0:T(8,128)} %broadcast_in_dim.15), calls=%async_computation.4 | async-start | bytes 2097152 | tf_op jit(solution)/shard_map/all_to_all | solution.py:45
  230.2 2.1 copy-start.1

commit v3 on v2

--- a/solution.py
+++ b/solution.py
@@ -10,9 +10,9 @@
 highest_precision = lax.Precision.HIGHEST
 
 
-def inverse_cholesky_kernel(inner_ref, inverse_ref):
-    size = inner_ref.shape[0]
-    schur = inner_ref[...]
+def inverse_cholesky(inner_gram):
+    size = inner_gram.shape[0]
+    schur = inner_gram
     rows = lax.broadcasted_iota(jnp.int32, (size, 1), 0)
     cols = lax.broadcasted_iota(jnp.int32, (1, size), 1)
     inverse = (rows == cols).astype(jnp.float32)
@@ -23,22 +23,44 @@
         schur = schur - factor_col * factor_row
         step = jnp.where(rows > j, factor_col * inv_pivot, jnp.where(rows == j, 1.0 - inv_pivot, 0.0))
         inverse = inverse - step * inverse[j:j + 1, :]
-    inverse_ref[...] = inverse
+    return inverse
 
 
-def inverse_cholesky(inner_gram):
-    return pl.pallas_call(
-        inverse_cholesky_kernel,
-        out_shape=jax.ShapeDtypeStruct(inner_gram.shape, jnp.float32),
-    )(inner_gram)
+def orthonormal_in_kernel(matrix):
+    inner_gram = jnp.dot(matrix.T, matrix, precision=highest_precision,
+                         preferred_element_type=jnp.float32)
+    lower_inverse = inverse_cholesky(inner_gram)
+    return lax.dot_general(
+        matrix, lower_inverse, (((1,), (1,)), ((), ())), precision=highest_precision,
+        preferred_element_type=jnp.float32,
+    )
+
+
+def orthonormal_kernel(block_ref, basis_ref):
+    basis_ref[...] = orthonormal_in_kernel(block_ref[...])
+
+
+def iterate_kernel(gram_ref, basis_ref, out_ref):
+    basis = basis_ref[...]
+    for iteration in range(ITERS):
+        product = jnp.dot(gram_ref[...], basis, precision=highest_precision,
+                          preferred_element_type=jnp.float32)
+        basis = orthonormal_in_kernel(product)
+    out_ref[...] = basis
 
 
 def orthonormal(matrix):
-    inner_gram = jnp.dot(matrix.T, matrix, precision=highest_precision)
-    lower_inverse = inverse_cholesky(inner_gram)
-    return lax.dot_general(
-        matrix, lower_inverse, (((1,), (1,)), ((), ())), precision=highest_precision
-    )
+    return pl.pallas_call(
+        orthonormal_kernel,
+        out_shape=jax.ShapeDtypeStruct(matrix.shape, jnp.float32),
+    )(matrix)
+
+
+def subspace_iteration(gram_matrix, mode_basis):
+    return pl.pallas_call(
+        iterate_kernel,
+        out_shape=jax.ShapeDtypeStruct(mode_basis.shape, jnp.float32),
+    )(gram_matrix, mode_basis)
 
 
 def exchange(blocks, axis):
@@ -70,8 +92,7 @@
     mode_basis = orthonormal(start_block)
     local_gram = jnp.dot(fibres, fibres.T, precision=highest_precision) / total_columns
     gram_matrix = all_reduce(local_gram)
-    for iteration in range(ITERS):
-        mode_basis = orthonormal(jnp.dot(gram_matrix, mode_basis, precision=highest_precision))
+    mode_basis = subspace_iteration(gram_matrix, mode_basis)
     core_tensor = jnp.dot(mode_basis.T, fibres, precision=highest_precision)
     return (mode_basis, core_tensor)
 

time: 234 us -> 232 us (level)
  matrix products: 16.6 us -> 6.65 us
  Pallas kernels: 26.6 us -> 33.1 us
  local copies, waits for them, and re-layouts: 2.99 us -> 5.55 us
    dot_general x11 -> x0, matrix products: 11 us -> none  [the longest x4 4.07 us: orthonormal(): lax.dot_general(matrix, lower_inverse, (((1,), (1,)), ((), ())), precisio...]
    pallas_call x4 -> x2, Pallas kernels: 26.6 us -> 33.1 us  [the longest x1 25.5 us: subspace_iteration(): pl.pallas_call(iterate_kernel, out_shape=jax.ShapeDtypeStruct(mode_basis....]
    unnamed x5 -> x9, local copies, waits for them, and re-layouts: 0.02 us -> 2.61 us
  transfers between devices with their start and end apart: 1 -> 1, of which waited for: 1 -> 1; matrix products, arithmetic and copies ran while one was open for 1% -> 0% of each run, Pallas kernels for 3% -> 3%
where the time goes in v3:
time: 232 us; the launch traced here: 231 us
  blocking collectives  175 us (75%)
  Pallas kernels  33.1 us (14%)
  matrix products  6.65 us (3%)
  waiting for transfers between devices  6.62 us (3%)
  local copies, waits for them, and re-layouts  5.55 us (2%)
  starting transfers between devices  3.83 us (2%)
    all_to_all x1, blocking collectives, on_device(): lax.all_to_all(species_field, 'fibre', split_axis=1, concat_axis=0, tiled...  117 us
    all_to_all x3, blocking collectives, exchange(): return lax.all_to_all(blocks, axis, 0, 0, tiled=True)  57.7 us
    pallas_call x1, Pallas kernels, subspace_iteration(): pl.pallas_call(iterate_kernel, out_shape=jax.ShapeDtypeStruct(mode_basis....  25.5 us
    pallas_call x1, Pallas kernels, orthonormal(): pl.pallas_call(orthonormal_kernel, out_shape=jax.ShapeDtypeStruct(matrix....  7.63 us
    all_to_all x1, waiting for transfers between devices, exchange(): return lax.all_to_all(blocks, axis, 0, 0, tiled=True)  6.62 us
  transfers between devices with their start and end apart: 1, of which 1 were waited for; matrix products, arithmetic and copies ran while one was open for 0% of the time, Pallas kernels for 3%

profile of v3, /device:TPU:1, one launch (start us, length us, event | category | flops | bytes accessed | tf_op | source)
XLA Modules:
  0.0 231.5 jit_solution(14586171094019084562)
XLA Ops:
  0.6 1.7 copy.18
  2.4 117.2 %all_to_all.39 = f32[16,32,1024]{2,0,1:T(8,128)S(1)} all-to-all(f32[16,32,1024]{2,0,1:T(8,128)S(1)} %bitcast.18), channel_id=1, replica_groups=mesh['fibre'=32,'group'=16] {'fibre'}, dimensions={1} | all-to-all | bytes 4194304 | tf_op jit(solution)/shard_map/all_to_all | solution.py:90
  119.6 3.5 %convolution_multiply_fusion = f32[512,512]{1,0:T(8,128)S(1)} fusion(f32[512,1024]{1,0:T(8,128)S(1)} %bitcast.16), kind=kOutput, calls=%fused_computation.1 | convolution fusion | flops 3221487616 | bytes 3145728 | tf_op jit(solution)/shard_map/dot_general | solution.py:93
  123.1 22.7 %all_to_all.40 = f32[16,32,512]{2,1,0:T(8,128)S(1)} all-to-all(f32[16,32,512]{2,1,0:T(8,128)S(1)} %bitcast.19), channel_id=1, replica_groups=mesh['fibre'=32,'group'=16] {'group'}, dimensions={0} | all-to-all | bytes 2097152 | tf_op jit(solution)/shard_map/all_to_all | solution.py:67
  145.8 0.1 reduce_sum.18
  145.9 0.0 copy-start.2
  146.0 17.6 %all_to_all.41 = f32[32,1,512]{2,1,0:T(1,128)S(1)} all-to-all(f32[32,1,512]{2,1,0:T(1,128)S(1)} %reshape.23), channel_id=1, replica_groups=mesh['fibre'=32,'group'=16] {'fibre'}, dimensions={0} | all-to-all | bytes 131072 | tf_op jit(solution)/shard_map/all_to_all | solution.py:67
  163.6 0.1 reduce_sum.19
  163.7 17.3 %all_to_all.42 = f32[32,1,512]{2,1,0:T(1,128)S(1)} all-to-all(f32[32,1,512]{2,1,0:T(1,128)S(1)} %broadcast_in_dim.6), channel_id=1, replica_groups=mesh['fibre'=32,'group'=16] {'fibre'}, dimensions={0} | all-to-all | bytes 131072 | tf_op jit(solution)/shard_map/all_to_all | solution.py:67
  181.0 1.1 broadcast_in_dim.15
  182.1 3.8 %all-to-all-start.4 = ((f32[16,32,512]{2,1,0:T(8,128)}), f32[16,32,512]{2,1,0:T(8,128)S(1)}, u32[]{:S(2)}, u32[]{:S(2)}) async-start(f32[16,32,512]{2,1,0:T(8,128)} %broadcast_in_dim.15), calls=%async_computation.4 | async-start | bytes 2097152 | tf_op jit(solution)/shard_map/all_to_all | solution.py:67
  186.0 0.0 copy-done.2
  186.0 0.8 copy.12.block_ref
  186.8 7.6 %shard_map.41.basis_ref = f32[512,64]{1,0:T(8,128)} custom-call(f32[512,64]{1,0:T(8,128)} %copy.12.block_ref), custom_call_target="tpu_custom_call" | custom-call | tf_op jit(solution)/shard_map/pallas_call | solution.py:53
  194.5 6.6 %all-to-all-done.4 = f32[16,32,512]{2,1,0:T(8,128)S(1)} async-done(((f32[16,32,512]{2,1,0:T(8,128)}), f32[16,32,512]{2,1,0:T(8,128)S(1)}, u32[]{:S(2)}, u32[]{:S(2)}) %all-to-all-start.4) | async-done | bytes 1048608 | tf_op jit(solution)/shard_map/all_to_all | solution.py:67
  201.1 0.0 copy-start
  201.1 1.0 copy-done
  202.1 25.5 %shard_map.42 = f32[512,64]{1,0:T(8,128)} custom-call(f32[512,512]{1,0:T(8,128)} %bitcast.20, f32[512,64]{1,0:T(8,128)} %shard_map.41.basis_ref), custom_call_target="tpu_custom_call" | custom-call | tf_op jit(solution)/shard_map/pallas_call | solution.py:60
  227.6 0.0 copy-start.1
  227.6 3.1 %fusion = f32[64,1024]{1,0:T(8,128)} fusion(f32[512,64]{1,0:T(8,128)} %shard_map.42, f32[512,1024]{1,0:T(8,128)S(1)} %bitcast.17), kind=kOutput, calls=%fused_computation.3 | convolution fusion | flops 402653184 | bytes 2490368 | tf_op jit(solution)/shard_map/dot_general | solution.py:96
  230.7 0.0 copy-done.1
  230.7 0.8 copy.13
  (3 shorter events, 0.1 us)
Async XLA Ops:
  145.9 40.1 %copy-start.2 = (f32[512,64]{0,1:T(8,128)S(1)}, f32[512,64]{0,1:T(8,128)}, u32[]{:S(2)}) copy-start(f32[512,64]{0,1:T(8,128)} %param.3) | copy-start | bytes 393220
  182.1 18.9 %all-to-all-start.4 = ((f32[16,32,512]{2,1,0:T(8,128)}), f32[16,32,512]{2,1,0:T(8,128)S(1)}, u32[]{:S(2)}, u32[]{:S(2)}) async-start(f32[16,32,512]{2,1,0:T(8,128)} %broadcast_in_dim.15), calls=%async_computation.4 | async-start | bytes 2097152 | tf_op jit(solution)/shard_map/all_to_all | solution.py:67
  201.1 1.0 copy-start
  227.6 3.1 %copy-start.1 = (f32[512,64]{1,0:T(8,128)S(1)}, f32[512,64]{1,0:T(8,128)}, u32[]{:S(2)}) copy-start(f32[512,64]{1,0:T(8,128)} %shard_map.42) | copy-start | bytes 393220

commit v4 on v3

--- a/solution.py
+++ b/solution.py
@@ -89,7 +89,7 @@
 def on_device(species_field, start_block):
     fibres = lax.all_to_all(species_field, "fibre", split_axis=1, concat_axis=0, tiled=True)
     total_columns = fibres.shape[1] * lax.axis_size("fibre") * lax.axis_size("group")
-    mode_basis = orthonormal(start_block)
+    fibres, mode_basis = lax.optimization_barrier((fibres, orthonormal(start_block)))
     local_gram = jnp.dot(fibres, fibres.T, precision=highest_precision) / total_columns
     gram_matrix = all_reduce(local_gram)
     mode_basis = subspace_iteration(gram_matrix, mode_basis)

time: 232 us -> 231 us (level)
  blocking collectives: 175 us -> 78.3 us
  waiting for transfers between devices: 6.62 us -> 90.1 us
  starting transfers between devices: 3.83 us -> 16.9 us
    all_to_all x1 -> x0, blocking collectives: 117 us -> none  [on_device(): lax.all_to_all(species_field, 'fibre', split_axis=1, concat_axis=0, tiled...]
    all_to_all x1, waiting for transfers between devices: 6.62 us -> 90.1 us  [on_device(): lax.all_to_all(species_field, 'fibre', split_axis=1, concat_axis=0, tiled...]
    all_to_all x3 -> x4, blocking collectives: 57.7 us -> 78.3 us  [exchange(): return lax.all_to_all(blocks, axis, 0, 0, tiled=True)]
    all_to_all x1, starting transfers between devices: 3.83 us -> 16.9 us  [on_device(): lax.all_to_all(species_field, 'fibre', split_axis=1, concat_axis=0, tiled...]
where the time goes in v4:
time: 231 us
  waiting for transfers between devices  90.1 us (39%)
  blocking collectives  78.3 us (34%)
  Pallas kernels  33.1 us (14%)
  starting transfers between devices  16.9 us (7%)
  matrix products  6.65 us (3%)
  local copies, waits for them, and re-layouts  5.02 us (2%)
    all_to_all x1, waiting for transfers between devices, on_device(): lax.all_to_all(species_field, 'fibre', split_axis=1, concat_axis=0, tiled...  90.1 us
    all_to_all x4, blocking collectives, exchange(): return lax.all_to_all(blocks, axis, 0, 0, tiled=True)  78.3 us
    pallas_call x1, Pallas kernels, subspace_iteration(): pl.pallas_call(iterate_kernel, out_shape=jax.ShapeDtypeStruct(mode_basis....  25.5 us
    all_to_all x1, starting transfers between devices, on_device(): lax.all_to_all(species_field, 'fibre', split_axis=1, concat_axis=0, tiled...  16.9 us
    pallas_call x1, Pallas kernels, orthonormal(): pl.pallas_call(orthonormal_kernel, out_shape=jax.ShapeDtypeStruct(matrix....  7.64 us
  transfers between devices with their start and end apart: 1, of which 1 were waited for; matrix products, arithmetic and copies ran while one was open for 0% of the time, Pallas kernels for 3%

profile of v4, /device:TPU:1, one launch (start us, length us, event | category | flops | bytes accessed | tf_op | source)
XLA Modules:
  0.0 230.9 jit_solution(6962002423677084123)
XLA Ops:
  0.6 3.2 %copy.18 = f32[2,32,8,1024]{3,2,0,1:T(8,128)} copy(f32[2,32,8,1024]{3,2,1,0:T(8,128)} %bitcast.21) | data formatting | bytes 4194304 | tf_op jit(solution)/shard_map/all_to_all | solution.py:90
  3.8 0.0 copy-start.1
  3.8 16.9 %all-to-all-start = ((f32[16,32,1024]{2,0,1:T(8,128)}), f32[16,32,1024]{2,0,1:T(8,128)S(1)}, u32[]{:S(2)}, u32[]{:S(2)}) async-start(f32[16,32,1024]{2,0,1:T(8,128)} %bitcast.18), calls=%async_computation | async-start | bytes 4194304 | tf_op jit(solution)/shard_map/all_to_all | solution.py:90
  20.7 0.0 copy-done.1
  20.7 0.8 copy.12.block_ref
  21.6 7.6 %shard_map.41.basis_ref = f32[512,64]{1,0:T(8,128)} custom-call(f32[512,64]{1,0:T(8,128)} %copy.12.block_ref), custom_call_target="tpu_custom_call" | custom-call | tf_op jit(solution)/shard_map/pallas_call | solution.py:53
  29.2 90.1 %all-to-all-done = f32[16,32,1024]{2,0,1:T(8,128)S(1)} async-done(((f32[16,32,1024]{2,0,1:T(8,128)}), f32[16,32,1024]{2,0,1:T(8,128)S(1)}, u32[]{:S(2)}, u32[]{:S(2)}) %all-to-all-start) | async-done | bytes 2097184 | tf_op jit(solution)/shard_map/all_to_all | solution.py:90
  119.3 3.5 %convolution_multiply_fusion = f32[512,512]{1,0:T(8,128)S(1)} fusion(f32[512,1024]{1,0:T(8,128)S(1)} %bitcast.16), kind=kOutput, calls=%fused_computation.1 | convolution fusion | flops 3221487616 | bytes 3145728 | tf_op jit(solution)/shard_map/dot_general | solution.py:93
  122.9 22.6 %all_to_all.39 = f32[16,32,512]{2,1,0:T(8,128)S(1)} all-to-all(f32[16,32,512]{2,1,0:T(8,128)S(1)} %bitcast.19), channel_id=1, replica_groups=mesh['fibre'=32,'group'=16] {'group'}, dimensions={0} | all-to-all | bytes 2097152 | tf_op jit(solution)/shard_map/all_to_all | solution.py:67
  145.5 0.1 reduce_sum.18
  145.6 19.4 %all_to_all.40 = f32[32,1,512]{2,1,0:T(1,128)S(1)} all-to-all(f32[32,1,512]{2,1,0:T(1,128)S(1)} %reshape.23), channel_id=1, replica_groups=mesh['fibre'=32,'group'=16] {'fibre'}, dimensions={0} | all-to-all | bytes 131072 | tf_op jit(solution)/shard_map/all_to_all | solution.py:67
  165.0 0.1 reduce_sum.19
  165.1 17.3 %all_to_all.41 = f32[32,1,512]{2,1,0:T(1,128)S(1)} all-to-all(f32[32,1,512]{2,1,0:T(1,128)S(1)} %broadcast_in_dim.6), channel_id=1, replica_groups=mesh['fibre'=32,'group'=16] {'fibre'}, dimensions={0} | all-to-all | bytes 131072 | tf_op jit(solution)/shard_map/all_to_all | solution.py:67
  182.4 0.1 broadcast_in_dim.15
  182.5 19.0 %all_to_all.42 = f32[16,32,512]{2,1,0:T(8,128)} all-to-all(f32[16,32,512]{2,1,0:T(8,128)S(1)} %broadcast_in_dim.15), channel_id=1, replica_groups=mesh['fibre'=32,'group'=16] {'group'}, dimensions={0} | all-to-all | bytes 2097152 | tf_op jit(solution)/shard_map/all_to_all | solution.py:67
  201.5 25.5 %shard_map.42 = f32[512,64]{1,0:T(8,128)} custom-call(f32[512,512]{1,0:T(8,128)} %bitcast.20, f32[512,64]{1,0:T(8,128)} %shard_map.41.basis_ref), custom_call_target="tpu_custom_call" | custom-call | tf_op jit(solution)/shard_map/pallas_call | solution.py:60
  227.0 0.0 copy-start
  227.0 3.1 %fusion = f32[64,1024]{1,0:T(8,128)} fusion(f32[512,64]{1,0:T(8,128)} %shard_map.42, f32[512,1024]{1,0:T(8,128)S(1)} %bitcast.17), kind=kOutput, calls=%fused_computation.3 | convolution fusion | flops 402653184 | bytes 2490368 | tf_op jit(solution)/shard_map/dot_general | solution.py:96
  230.2 0.0 copy-done
  230.2 0.8 copy.13
  (3 shorter events, 0.1 us)
Async XLA Ops:
  3.8 16.9 %copy-start.1 = (f32[512,64]{0,1:T(8,128)S(1)}, f32[512,64]{0,1:T(8,128)}, u32[]{:S(2)}) copy-start(f32[512,64]{0,1:T(8,128)} %param.3) | copy-start | bytes 393220
  3.8 115.5 %all-to-all-start = ((f32[16,32,1024]{2,0,1:T(8,128)}), f32[16,32,1024]{2,0,1:T(8,128)S(1)}, u32[]{:S(2)}, u32[]{:S(2)}) async-start(f32[16,32,1024]{2,0,1:T(8,128)} %bitcast.18), calls=%async_computation | async-start | bytes 4194304 | tf_op jit(solution)/shard_map/all_to_all | solution.py:90
  227.0 3.1 %copy-start = (f32[512,64]{1,0:T(8,128)S(1)}, f32[512,64]{1,0:T(8,128)}, u32[]{:S(2)}) copy-start(f32[512,64]{1,0:T(8,128)} %shard_map.42) | copy-start | bytes 393220

commit v5 on v4

--- a/solution.py
+++ b/solution.py
@@ -79,11 +79,44 @@
     return exchange(blocks, axis).reshape(parts * matrix.shape[0], *matrix.shape[1:])
 
 
+def pad_rows(matrix, rows):
+    return jnp.pad(matrix, ((0, rows - matrix.shape[0]), (0, 0)))
+
+
 def all_reduce(matrix):
-    rows = reduce_scatter(matrix, "group")
+    groups, fibres = lax.axis_size("group"), lax.axis_size("fibre")
+    rows = pad_rows(matrix, -(-matrix.shape[0] // groups) * groups)
+    rows = reduce_scatter(rows, "group")
+    chunk = rows.shape[0]
+    rows = pad_rows(rows, -(-chunk // fibres) * fibres)
     rows = reduce_scatter(rows, "fibre")
-    rows = gather(rows, "fibre")
-    return gather(rows, "group")
+    rows = gather(rows, "fibre")[:chunk]
+    return gather(rows, "group")[:matrix.shape[0]]
+
+
+def pack_symmetric(gram):
+    half = gram.shape[0] // 2
+    upper_left, upper_right, lower_right = gram[:half, :half], gram[:half, half:], gram[half:, half:]
+    index = jnp.arange(half)
+    on_or_above = index[:, None] <= index[None, :]
+    triangles = jnp.where(on_or_above, upper_left, lower_right)
+    diagonal = jnp.diagonal(lower_right)[None, :]
+    return jnp.concatenate([triangles, upper_right, diagonal], axis=0)
+
+
+def unpack_symmetric(packed):
+    half = packed.shape[1]
+    triangles, upper_right, diagonal = packed[:half], packed[half:2 * half], packed[2 * half]
+    index = jnp.arange(half)
+    on_or_above = index[:, None] <= index[None, :]
+    below = index[:, None] > index[None, :]
+    upper_left = jnp.where(on_or_above, triangles, triangles.T)
+    lower_right = jnp.where(below, triangles, triangles.T)
+    lower_right = jnp.where(index[:, None] == index[None, :], diagonal[None, :], lower_right)
+    return jnp.concatenate([
+        jnp.concatenate([upper_left, upper_right], axis=1),
+        jnp.concatenate([upper_right.T, lower_right], axis=1),
+    ], axis=0)
 
 
 def on_device(species_field, start_block):
@@ -91,7 +124,7 @@
     total_columns = fibres.shape[1] * lax.axis_size("fibre") * lax.axis_size("group")
     fibres, mode_basis = lax.optimization_barrier((fibres, orthonormal(start_block)))
     local_gram = jnp.dot(fibres, fibres.T, precision=highest_precision) / total_columns
-    gram_matrix = all_reduce(local_gram)
+    gram_matrix = unpack_symmetric(all_reduce(pack_symmetric(local_gram)))
     mode_basis = subspace_iteration(gram_matrix, mode_basis)
     core_tensor = jnp.dot(mode_basis.T, fibres, precision=highest_precision)
     return (mode_basis, core_tensor)

time: 231 us -> 228 us (0.987)
  blocking collectives: 78.3 us -> 68.7 us
  other arithmetic: 0.14 us -> 3.21 us
  local copies, waits for them, and re-layouts: 5.02 us -> 7.75 us
    all_to_all x4, blocking collectives: 78.3 us -> 68.7 us  [exchange(): return lax.all_to_all(blocks, axis, 0, 0, tiled=True)]
    gather x0 -> x1, local copies, waits for them, and re-layouts: none -> 2.34 us  [pack_symmetric(): diagonal = jnp.diagonal(lower_right)[None, :]]
where the time goes in v5:
time: 228 us; the launch traced here: 227 us
  waiting for transfers between devices  90.1 us (40%)
  blocking collectives  68.7 us (30%)
  Pallas kernels  33.1 us (15%)
  starting transfers between devices  16.9 us (7%)
  local copies, waits for them, and re-layouts  7.75 us (3%)
  matrix products  6.65 us (3%)
  other arithmetic  3.21 us (1%)
    all_to_all x1, waiting for transfers between devices, on_device(): lax.all_to_all(species_field, 'fibre', split_axis=1, concat_axis=0, tiled...  90.1 us
    all_to_all x4, blocking collectives, exchange(): return lax.all_to_all(blocks, axis, 0, 0, tiled=True)  68.7 us
    pallas_call x1, Pallas kernels, subspace_iteration(): pl.pallas_call(iterate_kernel, out_shape=jax.ShapeDtypeStruct(mode_basis....  25.5 us
    all_to_all x1, starting transfers between devices, on_device(): lax.all_to_all(species_field, 'fibre', split_axis=1, concat_axis=0, tiled...  16.9 us
    pallas_call x1, Pallas kernels, orthonormal(): pl.pallas_call(orthonormal_kernel, out_shape=jax.ShapeDtypeStruct(matrix....  7.65 us
  transfers between devices with their start and end apart: 1, of which 1 were waited for; matrix products, arithmetic and copies ran while one was open for 0% of the time, Pallas kernels for 3%

profile of v5, /device:TPU:1, one launch (start us, length us, event | category | flops | bytes accessed | tf_op | source)
XLA Modules:
  0.0 227.2 jit_solution(14964847176594330195)
XLA Ops:
  0.6 3.2 %copy.36 = f32[2,32,8,1024]{3,2,0,1:T(8,128)} copy(f32[2,32,8,1024]{3,2,1,0:T(8,128)} %bitcast.25) | data formatting | bytes 4194304 | tf_op jit(solution)/shard_map/all_to_all | solution.py:123
  3.8 0.0 copy-start.1
  3.8 16.9 %all-to-all-start = ((f32[16,32,1024]{2,0,1:T(8,128)}), f32[16,32,1024]{2,0,1:T(8,128)S(1)}, u32[]{:S(2)}, u32[]{:S(2)}) async-start(f32[16,32,1024]{2,0,1:T(8,128)} %bitcast.24), calls=%async_computation | async-start | bytes 4194304 | tf_op jit(solution)/shard_map/all_to_all | solution.py:123
  20.7 0.0 copy-done.1
  20.7 0.8 copy.28.block_ref
  21.6 7.7 %shard_map.41.basis_ref = f32[512,64]{1,0:T(8,128)} custom-call(f32[512,64]{1,0:T(8,128)} %copy.28.block_ref), custom_call_target="tpu_custom_call" | custom-call | tf_op jit(solution)/shard_map/pallas_call | solution.py:53
  29.2 90.1 %all-to-all-done = f32[16,32,1024]{2,0,1:T(8,128)S(1)} async-done(((f32[16,32,1024]{2,0,1:T(8,128)}), f32[16,32,1024]{2,0,1:T(8,128)S(1)}, u32[]{:S(2)}, u32[]{:S(2)}) %all-to-all-start) | async-done | bytes 2097184 | tf_op jit(solution)/shard_map/all_to_all | solution.py:123
  119.3 3.5 %convolution_multiply_fusion = f32[512,512]{1,0:T(8,128)S(1)} fusion(f32[512,1024]{1,0:T(8,128)S(1)} %bitcast.21), kind=kOutput, calls=%fused_computation.2 | convolution fusion | flops 3221487616 | bytes 3145728 | tf_op jit(solution)/shard_map/dot_general | solution.py:126
  122.8 0.1 slice_select_fusion
  122.9 2.3 %gather_fusion = f32[256]{0:T(256)S(1)} fusion(f32[256,256]{1,0:T(8,128)S(1)} %get-tuple-element.20, s32[256]{0:T(256)S(1)} %bitcast.23), kind=kCustom, calls=%fused_computation | custom fusion | bytes 4096 | tf_op jit(solution)/shard_map/jit(diagonal)/cond/branch_0_fun/gather | solution.py:103
  125.3 0.1 reshape.21
  125.4 18.1 %all_to_all.39 = f32[16,33,256]{2,1,0:T(8,128)S(1)} all-to-all(f32[16,33,256]{2,1,0:T(8,128)S(1)} %reshape.21), channel_id=1, replica_groups=mesh['fibre'=32,'group'=16] {'group'}, dimensions={0} | all-to-all | bytes 1081344 | tf_op jit(solution)/shard_map/all_to_all | solution.py:67
  143.6 19.7 %all_to_all.40 = f32[32,2,256]{2,1,0:T(2,128)S(1)} all-to-all(f32[32,2,256]{2,1,0:T(2,128)S(1)} %reshape.22), channel_id=1, replica_groups=mesh['fibre'=32,'group'=16] {'fibre'}, dimensions={0} | all-to-all | bytes 131072 | tf_op jit(solution)/shard_map/all_to_all | solution.py:67
  163.4 17.3 %all_to_all.41 = f32[32,2,256]{2,1,0:T(2,128)S(1)} all-to-all(f32[32,2,256]{2,1,0:T(2,128)S(1)} %broadcast_in_dim.18), channel_id=1, replica_groups=mesh['fibre'=32,'group'=16] {'fibre'}, dimensions={0} | all-to-all | bytes 131072 | tf_op jit(solution)/shard_map/all_to_all | solution.py:67
  180.8 13.7 %all_to_all.42 = f32[16,33,256]{2,1,0:T(8,128)S(1)} all-to-all(f32[16,33,256]{2,1,0:T(8,128)S(1)} %broadcast_in_dim.19), channel_id=1, replica_groups=mesh['fibre'=32,'group'=16] {'group'}, dimensions={0} | all-to-all | bytes 1081344 | tf_op jit(solution)/shard_map/all_to_all | solution.py:67
  194.4 0.1 reshape.24
  194.5 0.1 copy.30
  194.7 0.9 bitcast_select_fusion.1
  195.6 0.1 copy.31
  195.7 2.1 maximum_maximum_fusion.gram_ref
  197.8 25.5 %shard_map.42 = f32[512,64]{1,0:T(8,128)} custom-call(f32[512,512]{1,0:T(8,128)} %maximum_maximum_fusion.gram_ref, f32[512,64]{1,0:T(8,128)} %shard_map.41.basis_ref), custom_call_target="tpu_custom_call" | custom-call | tf_op jit(solution)/shard_map/pallas_call | solution.py:60
  223.3 0.0 copy-start
  223.3 3.1 %fusion.1 = f32[64,1024]{1,0:T(8,128)} fusion(f32[512,64]{1,0:T(8,128)} %shard_map.42, f32[512,1024]{1,0:T(8,128)S(1)} %bitcast.22), kind=kOutput, calls=%fused_computation.16 | convolution fusion | flops 402653184 | bytes 2490368 | tf_op jit(solution)/shard_map/dot_general | solution.py:129
  226.4 0.0 copy-done
  226.4 0.8 copy.32
  (12 shorter events, 0.3 us)
Async XLA Ops:
  3.8 16.9 %copy-start.1 = (f32[512,64]{0,1:T(8,128)S(1)}, f32[512,64]{0,1:T(8,128)}, u32[]{:S(2)}) copy-start(f32[512,64]{0,1:T(8,128)} %param.3) | copy-start | bytes 393220
  3.8 115.5 %all-to-all-start = ((f32[16,32,1024]{2,0,1:T(8,128)}), f32[16,32,1024]{2,0,1:T(8,128)S(1)}, u32[]{:S(2)}, u32[]{:S(2)}) async-start(f32[16,32,1024]{2,0,1:T(8,128)} %bitcast.24), calls=%async_computation | async-start | bytes 4194304 | tf_op jit(solution)/shard_map/all_to_all | solution.py:123
  223.3 3.1 %copy-start = (f32[512,64]{1,0:T(8,128)S(1)}, f32[512,64]{1,0:T(8,128)}, u32[]{:S(2)}) copy-start(f32[512,64]{1,0:T(8,128)} %shard_map.42) | copy-start | bytes 393220

commit v6 on v5

--- a/solution.py
+++ b/solution.py
@@ -12,18 +12,28 @@
 
 def inverse_cholesky(inner_gram):
     size = inner_gram.shape[0]
-    schur = inner_gram
-    rows = lax.broadcasted_iota(jnp.int32, (size, 1), 0)
+    count = size // 8
+    schur = [inner_gram[8 * b:8 * b + 8, :] for b in range(count)]
+    rows = lax.broadcasted_iota(jnp.int32, (8, 1), 0)
     cols = lax.broadcasted_iota(jnp.int32, (1, size), 1)
-    inverse = (rows == cols).astype(jnp.float32)
+    inverse = [((rows + 8 * b) == cols).astype(jnp.float32) for b in range(count)]
     for j in range(size):
-        inv_pivot = lax.rsqrt(schur[j:j + 1, j:j + 1])
-        factor_col = jnp.where(rows >= j, schur[:, j:j + 1] * inv_pivot, 0.0)
-        factor_row = jnp.where(cols >= j, schur[j:j + 1, :] * inv_pivot, 0.0)
-        schur = schur - factor_col * factor_row
-        step = jnp.where(rows > j, factor_col * inv_pivot, jnp.where(rows == j, 1.0 - inv_pivot, 0.0))
-        inverse = inverse - step * inverse[j:j + 1, :]
-    return inverse
+        pivot_block, r = divmod(j, 8)
+        pivot_row = schur[pivot_block][r:r + 1, :]
+        inv_pivot = lax.rsqrt(pivot_row[:, j:j + 1])
+        recip = inv_pivot * inv_pivot
+        scaled_row = jnp.where(cols >= j, pivot_row, 0.0) * recip
+        inverse_row = inverse[pivot_block][r:r + 1, :]
+        for b in range(pivot_block, count):
+            col = schur[b][:, j:j + 1]
+            if b == pivot_block:
+                col = jnp.where(rows >= r, col, 0.0)
+                step = jnp.where(rows > r, col * recip, jnp.where(rows == r, 1.0 - inv_pivot, 0.0))
+            else:
+                step = col * recip
+            schur[b] = schur[b] - col * scaled_row
+            inverse[b] = inverse[b] - step * inverse_row
+    return jnp.concatenate(inverse, axis=0)
 
 
 def orthonormal_in_kernel(matrix):

time: 228 us -> 228 us (level)
  no operation moved by 1% of the time
where the time goes in v6:
time: 228 us; the launch traced here: 227 us
  waiting for transfers between devices  90 us (39%)
  blocking collectives  68.7 us (30%)
  Pallas kernels  33 us (14%)
  starting transfers between devices  16.9 us (7%)
  local copies, waits for them, and re-layouts  7.75 us (3%)
  matrix products  6.65 us (3%)
  other arithmetic  3.21 us (1%)
    all_to_all x1, waiting for transfers between devices, on_device(): lax.all_to_all(species_field, 'fibre', split_axis=1, concat_axis=0, tiled...  90 us
    all_to_all x4, blocking collectives, exchange(): return lax.all_to_all(blocks, axis, 0, 0, tiled=True)  68.7 us
    pallas_call x1, Pallas kernels, subspace_iteration(): pl.pallas_call(iterate_kernel, out_shape=jax.ShapeDtypeStruct(mode_basis....  25.3 us
    all_to_all x1, starting transfers between devices, on_device(): lax.all_to_all(species_field, 'fibre', split_axis=1, concat_axis=0, tiled...  16.9 us
    pallas_call x1, Pallas kernels, orthonormal(): pl.pallas_call(orthonormal_kernel, out_shape=jax.ShapeDtypeStruct(matrix....  7.73 us
  transfers between devices with their start and end apart: 1, of which 1 were waited for; matrix products, arithmetic and copies ran while one was open for 0% of the time, Pallas kernels for 3%

profile of v6, /device:TPU:1, one launch (start us, length us, event | category | flops | bytes accessed | tf_op | source)
XLA Modules:
  0.0 227.0 jit_solution(17806980391677774487)
XLA Ops:
  0.6 3.2 %copy.36 = f32[2,32,8,1024]{3,2,0,1:T(8,128)} copy(f32[2,32,8,1024]{3,2,1,0:T(8,128)} %bitcast.25) | data formatting | bytes 4194304 | tf_op jit(solution)/shard_map/all_to_all | solution.py:133
  3.8 0.0 copy-start.1
  3.8 16.9 %all-to-all-start = ((f32[16,32,1024]{2,0,1:T(8,128)}), f32[16,32,1024]{2,0,1:T(8,128)S(1)}, u32[]{:S(2)}, u32[]{:S(2)}) async-start(f32[16,32,1024]{2,0,1:T(8,128)} %bitcast.24), calls=%async_computation | async-start | bytes 4194304 | tf_op jit(solution)/shard_map/all_to_all | solution.py:133
  20.7 0.0 copy-done.1
  20.7 0.8 copy.28.block_ref
  21.6 7.7 %shard_map.41.basis_ref = f32[512,64]{1,0:T(8,128)} custom-call(f32[512,64]{1,0:T(8,128)} %copy.28.block_ref), custom_call_target="tpu_custom_call" | custom-call | tf_op jit(solution)/shard_map/pallas_call | solution.py:63
  29.3 90.0 %all-to-all-done = f32[16,32,1024]{2,0,1:T(8,128)S(1)} async-done(((f32[16,32,1024]{2,0,1:T(8,128)}), f32[16,32,1024]{2,0,1:T(8,128)S(1)}, u32[]{:S(2)}, u32[]{:S(2)}) %all-to-all-start) | async-done | bytes 2097184 | tf_op jit(solution)/shard_map/all_to_all | solution.py:133
  119.3 3.5 %convolution_multiply_fusion = f32[512,512]{1,0:T(8,128)S(1)} fusion(f32[512,1024]{1,0:T(8,128)S(1)} %bitcast.21), kind=kOutput, calls=%fused_computation.2 | convolution fusion | flops 3221487616 | bytes 3145728 | tf_op jit(solution)/shard_map/dot_general | solution.py:136
  122.8 0.1 slice_select_fusion
  122.9 2.3 %gather_fusion = f32[256]{0:T(256)S(1)} fusion(f32[256,256]{1,0:T(8,128)S(1)} %get-tuple-element.20, s32[256]{0:T(256)S(1)} %bitcast.23), kind=kCustom, calls=%fused_computation | custom fusion | bytes 4096 | tf_op jit(solution)/shard_map/jit(diagonal)/cond/branch_0_fun/gather | solution.py:113
  125.3 0.1 reshape.21
  125.4 18.1 %all_to_all.39 = f32[16,33,256]{2,1,0:T(8,128)S(1)} all-to-all(f32[16,33,256]{2,1,0:T(8,128)S(1)} %reshape.21), channel_id=1, replica_groups=mesh['fibre'=32,'group'=16] {'group'}, dimensions={0} | all-to-all | bytes 1081344 | tf_op jit(solution)/shard_map/all_to_all | solution.py:77
  143.6 19.7 %all_to_all.40 = f32[32,2,256]{2,1,0:T(2,128)S(1)} all-to-all(f32[32,2,256]{2,1,0:T(2,128)S(1)} %reshape.22), channel_id=1, replica_groups=mesh['fibre'=32,'group'=16] {'fibre'}, dimensions={0} | all-to-all | bytes 131072 | tf_op jit(solution)/shard_map/all_to_all | solution.py:77
  163.4 17.3 %all_to_all.41 = f32[32,2,256]{2,1,0:T(2,128)S(1)} all-to-all(f32[32,2,256]{2,1,0:T(2,128)S(1)} %broadcast_in_dim.18), channel_id=1, replica_groups=mesh['fibre'=32,'group'=16] {'fibre'}, dimensions={0} | all-to-all | bytes 131072 | tf_op jit(solution)/shard_map/all_to_all | solution.py:77
  180.8 13.7 %all_to_all.42 = f32[16,33,256]{2,1,0:T(8,128)S(1)} all-to-all(f32[16,33,256]{2,1,0:T(8,128)S(1)} %broadcast_in_dim.19), channel_id=1, replica_groups=mesh['fibre'=32,'group'=16] {'group'}, dimensions={0} | all-to-all | bytes 1081344 | tf_op jit(solution)/shard_map/all_to_all | solution.py:77
  194.4 0.1 reshape.24
  194.5 0.1 copy.30
  194.7 0.9 bitcast_select_fusion.1
  195.6 0.1 copy.31
  195.7 2.1 maximum_maximum_fusion.gram_ref
  197.8 25.3 %shard_map.42 = f32[512,64]{1,0:T(8,128)} custom-call(f32[512,512]{1,0:T(8,128)} %maximum_maximum_fusion.gram_ref, f32[512,64]{1,0:T(8,128)} %shard_map.41.basis_ref), custom_call_target="tpu_custom_call" | custom-call | tf_op jit(solution)/shard_map/pallas_call | solution.py:70
  223.1 0.0 copy-start
  223.1 3.1 %fusion.1 = f32[64,1024]{1,0:T(8,128)} fusion(f32[512,64]{1,0:T(8,128)} %shard_map.42, f32[512,1024]{1,0:T(8,128)S(1)} %bitcast.22), kind=kOutput, calls=%fused_computation.16 | convolution fusion | flops 402653184 | bytes 2490368 | tf_op jit(solution)/shard_map/dot_general | solution.py:139
  226.2 0.0 copy-done
  226.2 0.8 copy.32
  (12 shorter events, 0.3 us)
Async XLA Ops:
  3.8 16.9 %copy-start.1 = (f32[512,64]{0,1:T(8,128)S(1)}, f32[512,64]{0,1:T(8,128)}, u32[]{:S(2)}) copy-start(f32[512,64]{0,1:T(8,128)} %param.3) | copy-start | bytes 393220
  3.8 115.5 %all-to-all-start = ((f32[16,32,1024]{2,0,1:T(8,128)}), f32[16,32,1024]{2,0,1:T(8,128)S(1)}, u32[]{:S(2)}, u32[]{:S(2)}) async-start(f32[16,32,1024]{2,0,1:T(8,128)} %bitcast.24), calls=%async_computation | async-start | bytes 4194304 | tf_op jit(solution)/shard_map/all_to_all | solution.py:133
  223.1 3.1 %copy-start = (f32[512,64]{1,0:T(8,128)S(1)}, f32[512,64]{1,0:T(8,128)}, u32[]{:S(2)}) copy-start(f32[512,64]{1,0:T(8,128)} %shard_map.42) | copy-start | bytes 393220

commit v7 on v6

--- a/solution.py
+++ b/solution.py
@@ -8,6 +8,7 @@
 
 
 highest_precision = lax.Precision.HIGHEST
+product_precision = lax.Precision.HIGH
 
 
 def inverse_cholesky(inner_gram):
@@ -53,7 +54,7 @@
 def iterate_kernel(gram_ref, basis_ref, out_ref):
     basis = basis_ref[...]
     for iteration in range(ITERS):
-        product = jnp.dot(gram_ref[...], basis, precision=highest_precision,
+        product = jnp.dot(gram_ref[...], basis, precision=product_precision,
                           preferred_element_type=jnp.float32)
         basis = orthonormal_in_kernel(product)
     out_ref[...] = basis
@@ -133,10 +134,10 @@
     fibres = lax.all_to_all(species_field, "fibre", split_axis=1, concat_axis=0, tiled=True)
     total_columns = fibres.shape[1] * lax.axis_size("fibre") * lax.axis_size("group")
     fibres, mode_basis = lax.optimization_barrier((fibres, orthonormal(start_block)))
-    local_gram = jnp.dot(fibres, fibres.T, precision=highest_precision) / total_columns
+    local_gram = jnp.dot(fibres, fibres.T, precision=product_precision) / total_columns
     gram_matrix = unpack_symmetric(all_reduce(pack_symmetric(local_gram)))
     mode_basis = subspace_iteration(gram_matrix, mode_basis)
-    core_tensor = jnp.dot(mode_basis.T, fibres, precision=highest_precision)
+    core_tensor = jnp.dot(mode_basis.T, fibres, precision=product_precision)
     return (mode_basis, core_tensor)
 
 

time: 228 us -> 224 us (0.982)
  matrix products: 6.65 us -> 4.35 us
    dot_general x2, matrix products: 6.65 us -> 4.35 us  [the longest x1 2.51 us: on_device(): core_tensor = jnp.dot(mode_basis.T, fibres, precision=product_precision)]
where the time goes in v7:
time: 224 us; the launch traced here: 223 us
  waiting for transfers between devices  90 us (40%)
  blocking collectives  68.7 us (31%)
  Pallas kernels  31 us (14%)
  starting transfers between devices  16.9 us (8%)
  local copies, waits for them, and re-layouts  7.75 us (3%)
  matrix products  4.35 us (2%)
  other arithmetic  3.21 us (1%)
    all_to_all x1, waiting for transfers between devices, on_device(): lax.all_to_all(species_field, 'fibre', split_axis=1, concat_axis=0, tiled...  90 us
    all_to_all x4, blocking collectives, exchange(): return lax.all_to_all(blocks, axis, 0, 0, tiled=True)  68.7 us
    pallas_call x1, Pallas kernels, subspace_iteration(): pl.pallas_call(iterate_kernel, out_shape=jax.ShapeDtypeStruct(mode_basis....  23.2 us
    all_to_all x1, starting transfers between devices, on_device(): lax.all_to_all(species_field, 'fibre', split_axis=1, concat_axis=0, tiled...  16.9 us
    pallas_call x1, Pallas kernels, orthonormal(): pl.pallas_call(orthonormal_kernel, out_shape=jax.ShapeDtypeStruct(matrix....  7.73 us
  transfers between devices with their start and end apart: 1, of which 1 were waited for; matrix products, arithmetic and copies ran while one was open for 0% of the time, Pallas kernels for 3%

profile of v7, /device:TPU:1, one launch (start us, length us, event | category | flops | bytes accessed | tf_op | source)
XLA Modules:
  0.0 222.7 jit_solution(15431291056900881701)
XLA Ops:
  0.6 3.2 %copy.36 = f32[2,32,8,1024]{3,2,0,1:T(8,128)} copy(f32[2,32,8,1024]{3,2,1,0:T(8,128)} %bitcast.25) | data formatting | bytes 4194304 | tf_op jit(solution)/shard_map/all_to_all | solution.py:134
  3.8 0.0 copy-start.1
  3.8 16.9 %all-to-all-start = ((f32[16,32,1024]{2,0,1:T(8,128)}), f32[16,32,1024]{2,0,1:T(8,128)S(1)}, u32[]{:S(2)}, u32[]{:S(2)}) async-start(f32[16,32,1024]{2,0,1:T(8,128)} %bitcast.24), calls=%async_computation | async-start | bytes 4194304 | tf_op jit(solution)/shard_map/all_to_all | solution.py:134
  20.7 0.0 copy-done.1
  20.7 0.8 copy.28.block_ref
  21.6 7.7 %shard_map.41.basis_ref = f32[512,64]{1,0:T(8,128)} custom-call(f32[512,64]{1,0:T(8,128)} %copy.28.block_ref), custom_call_target="tpu_custom_call" | custom-call | tf_op jit(solution)/shard_map/pallas_call | solution.py:64
  29.3 90.0 %all-to-all-done = f32[16,32,1024]{2,0,1:T(8,128)S(1)} async-done(((f32[16,32,1024]{2,0,1:T(8,128)}), f32[16,32,1024]{2,0,1:T(8,128)S(1)}, u32[]{:S(2)}, u32[]{:S(2)}) %all-to-all-start) | async-done | bytes 2097184 | tf_op jit(solution)/shard_map/all_to_all | solution.py:134
  119.3 1.8 convolution_multiply_fusion
  121.2 0.1 slice_select_fusion
  121.2 2.3 %gather_fusion = f32[256]{0:T(256)S(1)} fusion(f32[256,256]{1,0:T(8,128)S(1)} %get-tuple-element.20, s32[256]{0:T(256)S(1)} %bitcast.23), kind=kCustom, calls=%fused_computation | custom fusion | bytes 4096 | tf_op jit(solution)/shard_map/jit(diagonal)/cond/branch_0_fun/gather | solution.py:114
  123.6 0.1 reshape.21
  123.7 18.1 %all_to_all.39 = f32[16,33,256]{2,1,0:T(8,128)S(1)} all-to-all(f32[16,33,256]{2,1,0:T(8,128)S(1)} %reshape.21), channel_id=1, replica_groups=mesh['fibre'=32,'group'=16] {'group'}, dimensions={0} | all-to-all | bytes 1081344 | tf_op jit(solution)/shard_map/all_to_all | solution.py:78
  141.9 19.7 %all_to_all.40 = f32[32,2,256]{2,1,0:T(2,128)S(1)} all-to-all(f32[32,2,256]{2,1,0:T(2,128)S(1)} %reshape.22), channel_id=1, replica_groups=mesh['fibre'=32,'group'=16] {'fibre'}, dimensions={0} | all-to-all | bytes 131072 | tf_op jit(solution)/shard_map/all_to_all | solution.py:78
  161.7 17.3 %all_to_all.41 = f32[32,2,256]{2,1,0:T(2,128)S(1)} all-to-all(f32[32,2,256]{2,1,0:T(2,128)S(1)} %broadcast_in_dim.18), channel_id=1, replica_groups=mesh['fibre'=32,'group'=16] {'fibre'}, dimensions={0} | all-to-all | bytes 131072 | tf_op jit(solution)/shard_map/all_to_all | solution.py:78
  179.1 13.7 %all_to_all.42 = f32[16,33,256]{2,1,0:T(8,128)S(1)} all-to-all(f32[16,33,256]{2,1,0:T(8,128)S(1)} %broadcast_in_dim.19), channel_id=1, replica_groups=mesh['fibre'=32,'group'=16] {'group'}, dimensions={0} | all-to-all | bytes 1081344 | tf_op jit(solution)/shard_map/all_to_all | solution.py:78
  192.7 0.1 reshape.24
  192.9 0.1 copy.30
  193.0 0.9 bitcast_select_fusion.1
  193.9 0.1 copy.31
  194.0 2.1 maximum_maximum_fusion.gram_ref
  196.2 23.2 %shard_map.42 = f32[512,64]{1,0:T(8,128)} custom-call(f32[512,512]{1,0:T(8,128)} %maximum_maximum_fusion.gram_ref, f32[512,64]{1,0:T(8,128)} %shard_map.41.basis_ref), custom_call_target="tpu_custom_call" | custom-call | tf_op jit(solution)/shard_map/pallas_call | solution.py:71
  219.4 0.0 copy-start
  219.4 2.5 %fusion.1 = f32[64,1024]{1,0:T(8,128)} fusion(f32[512,64]{1,0:T(8,128)} %shard_map.42, f32[512,1024]{1,0:T(8,128)S(1)} %bitcast.22), kind=kOutput, calls=%fused_computation.16 | convolution fusion | flops 201326592 | bytes 2490368 | tf_op jit(solution)/shard_map/dot_general | solution.py:140
  221.9 0.0 copy-done
  221.9 0.8 copy.32
  (12 shorter events, 0.3 us)
Async XLA Ops:
  3.8 16.9 %copy-start.1 = (f32[512,64]{0,1:T(8,128)S(1)}, f32[512,64]{0,1:T(8,128)}, u32[]{:S(2)}) copy-start(f32[512,64]{0,1:T(8,128)} %param.3) | copy-start | bytes 393220
  3.8 115.5 %all-to-all-start = ((f32[16,32,1024]{2,0,1:T(8,128)}), f32[16,32,1024]{2,0,1:T(8,128)S(1)}, u32[]{:S(2)}, u32[]{:S(2)}) async-start(f32[16,32,1024]{2,0,1:T(8,128)} %bitcast.24), calls=%async_computation | async-start | bytes 4194304 | tf_op jit(solution)/shard_map/all_to_all | solution.py:134
  219.4 2.5 %copy-start = (f32[512,64]{1,0:T(8,128)S(1)}, f32[512,64]{1,0:T(8,128)}, u32[]{:S(2)}) copy-start(f32[512,64]{1,0:T(8,128)} %shard_map.42) | copy-start | bytes 393220

commit v8 on v7

--- a/solution.py
+++ b/solution.py
@@ -51,11 +51,23 @@
     basis_ref[...] = orthonormal_in_kernel(block_ref[...])
 
 
-def iterate_kernel(gram_ref, basis_ref, out_ref):
+def split_bf16(matrix):
+    high = lax.reduce_precision(matrix, exponent_bits=8, mantissa_bits=7)
+    return high.astype(jnp.bfloat16), (matrix - high).astype(jnp.bfloat16)
+
+
+def three_pass_dot(left_high, left_low, right):
+    right_high, right_low = split_bf16(right)
+    product = jnp.dot(left_high, right_high, preferred_element_type=jnp.float32)
+    product += jnp.dot(left_high, right_low, preferred_element_type=jnp.float32)
+    product += jnp.dot(left_low, right_high, preferred_element_type=jnp.float32)
+    return product
+
+
+def iterate_kernel(gram_high_ref, gram_low_ref, basis_ref, out_ref):
     basis = basis_ref[...]
     for iteration in range(ITERS):
-        product = jnp.dot(gram_ref[...], basis, precision=product_precision,
-                          preferred_element_type=jnp.float32)
+        product = three_pass_dot(gram_high_ref[...], gram_low_ref[...], basis)
         basis = orthonormal_in_kernel(product)
     out_ref[...] = basis
 
@@ -68,10 +80,11 @@
 
 
 def subspace_iteration(gram_matrix, mode_basis):
+    gram_high, gram_low = split_bf16(gram_matrix)
     return pl.pallas_call(
         iterate_kernel,
         out_shape=jax.ShapeDtypeStruct(mode_basis.shape, jnp.float32),
-    )(gram_matrix, mode_basis)
+    )(gram_high, gram_low, mode_basis)
 
 
 def exchange(blocks, axis):

time: 224 us -> 224 us (level)
  no operation moved by 1% of the time
where the time goes in v8:
time: 224 us; the launch traced here: 223 us
  waiting for transfers between devices  90 us (40%)
  blocking collectives  68.7 us (31%)
  Pallas kernels  31 us (14%)
  starting transfers between devices  16.9 us (8%)
  local copies, waits for them, and re-layouts  7.74 us (3%)
  matrix products  4.35 us (2%)
  other arithmetic  3.23 us (1%)
    all_to_all x1, waiting for transfers between devices, on_device(): lax.all_to_all(species_field, 'fibre', split_axis=1, concat_axis=0, tiled...  90 us
    all_to_all x4, blocking collectives, exchange(): return lax.all_to_all(blocks, axis, 0, 0, tiled=True)  68.7 us
    pallas_call x1, Pallas kernels, subspace_iteration(): pl.pallas_call(iterate_kernel, out_shape=jax.ShapeDtypeStruct(mode_basis....  23.3 us
    all_to_all x1, starting transfers between devices, on_device(): lax.all_to_all(species_field, 'fibre', split_axis=1, concat_axis=0, tiled...  16.9 us
    pallas_call x1, Pallas kernels, orthonormal(): pl.pallas_call(orthonormal_kernel, out_shape=jax.ShapeDtypeStruct(matrix....  7.72 us
  transfers between devices with their start and end apart: 1, of which 1 were waited for; matrix products, arithmetic and copies ran while one was open for 0% of the time, Pallas kernels for 3%

profile of v8, /device:TPU:1, one launch (start us, length us, event | category | flops | bytes accessed | tf_op | source)
XLA Modules:
  0.0 222.7 jit_solution(2709168387177012297)
XLA Ops:
  0.6 3.2 %copy.36 = f32[2,32,8,1024]{3,2,0,1:T(8,128)} copy(f32[2,32,8,1024]{3,2,1,0:T(8,128)} %bitcast.25) | data formatting | bytes 4194304 | tf_op jit(solution)/shard_map/all_to_all | solution.py:147
  3.8 0.0 copy-start.1
  3.8 16.9 %all-to-all-start = ((f32[16,32,1024]{2,0,1:T(8,128)}), f32[16,32,1024]{2,0,1:T(8,128)S(1)}, u32[]{:S(2)}, u32[]{:S(2)}) async-start(f32[16,32,1024]{2,0,1:T(8,128)} %bitcast.24), calls=%async_computation | async-start | bytes 4194304 | tf_op jit(solution)/shard_map/all_to_all | solution.py:147
  20.7 0.0 copy-done.1
  20.7 0.8 copy.28.block_ref
  21.6 7.7 %shard_map.41.basis_ref = f32[512,64]{1,0:T(8,128)} custom-call(f32[512,64]{1,0:T(8,128)} %copy.28.block_ref), custom_call_target="tpu_custom_call" | custom-call | tf_op jit(solution)/shard_map/pallas_call | solution.py:76
  29.3 90.0 %all-to-all-done = f32[16,32,1024]{2,0,1:T(8,128)S(1)} async-done(((f32[16,32,1024]{2,0,1:T(8,128)}), f32[16,32,1024]{2,0,1:T(8,128)S(1)}, u32[]{:S(2)}, u32[]{:S(2)}) %all-to-all-start) | async-done | bytes 2097184 | tf_op jit(solution)/shard_map/all_to_all | solution.py:147
  119.3 1.8 convolution_multiply_fusion
  121.2 0.1 slice_select_fusion
  121.2 2.3 %gather_fusion = f32[256]{0:T(256)S(1)} fusion(f32[256,256]{1,0:T(8,128)S(1)} %get-tuple-element.22, s32[256]{0:T(256)S(1)} %bitcast.23), kind=kCustom, calls=%fused_computation | custom fusion | bytes 4096 | tf_op jit(solution)/shard_map/jit(diagonal)/cond/branch_0_fun/gather | solution.py:127
  123.6 0.1 reshape.21
  123.7 18.1 %all_to_all.39 = f32[16,33,256]{2,1,0:T(8,128)S(1)} all-to-all(f32[16,33,256]{2,1,0:T(8,128)S(1)} %reshape.21), channel_id=1, replica_groups=mesh['fibre'=32,'group'=16] {'group'}, dimensions={0} | all-to-all | bytes 1081344 | tf_op jit(solution)/shard_map/all_to_all | solution.py:91
  141.9 19.7 %all_to_all.40 = f32[32,2,256]{2,1,0:T(2,128)S(1)} all-to-all(f32[32,2,256]{2,1,0:T(2,128)S(1)} %reshape.22), channel_id=1, replica_groups=mesh['fibre'=32,'group'=16] {'fibre'}, dimensions={0} | all-to-all | bytes 131072 | tf_op jit(solution)/shard_map/all_to_all | solution.py:91
  161.7 17.3 %all_to_all.41 = f32[32,2,256]{2,1,0:T(2,128)S(1)} all-to-all(f32[32,2,256]{2,1,0:T(2,128)S(1)} %broadcast_in_dim.18), channel_id=1, replica_groups=mesh['fibre'=32,'group'=16] {'fibre'}, dimensions={0} | all-to-all | bytes 131072 | tf_op jit(solution)/shard_map/all_to_all | solution.py:91
  179.1 13.7 %all_to_all.42 = f32[16,33,256]{2,1,0:T(8,128)S(1)} all-to-all(f32[16,33,256]{2,1,0:T(8,128)S(1)} %broadcast_in_dim.19), channel_id=1, replica_groups=mesh['fibre'=32,'group'=16] {'group'}, dimensions={0} | all-to-all | bytes 1081344 | tf_op jit(solution)/shard_map/all_to_all | solution.py:91
  192.7 0.1 reshape.24
  192.9 0.1 copy.30
  193.0 0.9 bitcast_select_fusion.1
  193.9 0.1 copy.31
  194.0 2.1 fusion
  196.2 23.3 %shard_map.42 = f32[512,64]{1,0:T(8,128)} custom-call(bf16[512,512]{1,0:T(8,128)(2,1)} %get-tuple-element.19.gram_high_ref, bf16[512,512]{1,0:T(8,128)(2,1)} %get-tuple-element.18.gram_low_ref, f32[512,64]{1,0:T(8,128)} %shard_map.41.basis_ref), custom_call_target="tpu_custom_call" | custom-call | tf_op jit(solution)/shard_map/pallas_call | solution.py:84
  219.5 0.0 copy-start
  219.5 2.5 %fusion.2 = f32[64,1024]{1,0:T(8,128)} fusion(f32[512,64]{1,0:T(8,128)} %shard_map.42, f32[512,1024]{1,0:T(8,128)S(1)} %bitcast.22), kind=kOutput, calls=%fused_computation.19 | convolution fusion | flops 201326592 | bytes 2490368 | tf_op jit(solution)/shard_map/dot_general | solution.py:153
  222.0 0.0 copy-done
  222.0 0.8 copy.32
  (12 shorter events, 0.3 us)
Async XLA Ops:
  3.8 16.9 %copy-start.1 = (f32[512,64]{0,1:T(8,128)S(1)}, f32[512,64]{0,1:T(8,128)}, u32[]{:S(2)}) copy-start(f32[512,64]{0,1:T(8,128)} %param.3) | copy-start | bytes 393220
  3.8 115.5 %all-to-all-start = ((f32[16,32,1024]{2,0,1:T(8,128)}), f32[16,32,1024]{2,0,1:T(8,128)S(1)}, u32[]{:S(2)}, u32[]{:S(2)}) async-start(f32[16,32,1024]{2,0,1:T(8,128)} %bitcast.24), calls=%async_computation | async-start | bytes 4194304 | tf_op jit(solution)/shard_map/all_to_all | solution.py:147
  219.5 2.5 %copy-start = (f32[512,64]{1,0:T(8,128)S(1)}, f32[512,64]{1,0:T(8,128)}, u32[]{:S(2)}) copy-start(f32[512,64]{1,0:T(8,128)} %shard_map.42) | copy-start | bytes 393220

commit v9 on v7

--- a/solution.py
+++ b/solution.py
@@ -2,6 +2,7 @@
 import jax.numpy as jnp
 from jax import lax
 from jax.experimental import pallas as pl
+from jax.experimental.pallas import tpu as pltpu
 from jax.sharding import PartitionSpec as P
 
 ITERS = 3
@@ -51,7 +52,19 @@
     basis_ref[...] = orthonormal_in_kernel(block_ref[...])
 
 
-def iterate_kernel(gram_ref, basis_ref, out_ref):
+def iterate_kernel(packed_ref, basis_ref, out_ref, gram_ref):
+    half = packed_ref.shape[1]
+    triangles = packed_ref[0:half, :]
+    upper_right = packed_ref[half:2 * half, :]
+    diagonal = packed_ref[2 * half:2 * half + 1, :]
+    rows = lax.broadcasted_iota(jnp.int32, (half, 1), 0)
+    cols = lax.broadcasted_iota(jnp.int32, (1, half), 1)
+    mirrored = triangles.T
+    gram_ref[0:half, 0:half] = jnp.where(rows <= cols, triangles, mirrored)
+    lower_right = jnp.where(rows > cols, triangles, mirrored)
+    gram_ref[half:, half:] = jnp.where(rows == cols, diagonal, lower_right)
+    gram_ref[0:half, half:] = upper_right
+    gram_ref[half:, 0:half] = upper_right.T
     basis = basis_ref[...]
     for iteration in range(ITERS):
         product = jnp.dot(gram_ref[...], basis, precision=product_precision,
@@ -67,11 +80,13 @@
     )(matrix)
 
 
-def subspace_iteration(gram_matrix, mode_basis):
+def subspace_iteration(packed_gram, mode_basis):
+    size = 2 * packed_gram.shape[1]
     return pl.pallas_call(
         iterate_kernel,
         out_shape=jax.ShapeDtypeStruct(mode_basis.shape, jnp.float32),
-    )(gram_matrix, mode_basis)
+        scratch_shapes=[pltpu.VMEM((size, size), jnp.float32)],
+    )(packed_gram, mode_basis)
 
 
 def exchange(blocks, axis):
@@ -102,7 +117,7 @@
     rows = pad_rows(rows, -(-chunk // fibres) * fibres)
     rows = reduce_scatter(rows, "fibre")
     rows = gather(rows, "fibre")[:chunk]
-    return gather(rows, "group")[:matrix.shape[0]]
+    return gather(rows, "group")
 
 
 def pack_symmetric(gram):
@@ -115,28 +130,13 @@
     return jnp.concatenate([triangles, upper_right, diagonal], axis=0)
 
 
-def unpack_symmetric(packed):
-    half = packed.shape[1]
-    triangles, upper_right, diagonal = packed[:half], packed[half:2 * half], packed[2 * half]
-    index = jnp.arange(half)
-    on_or_above = index[:, None] <= index[None, :]
-    below = index[:, None] > index[None, :]
-    upper_left = jnp.where(on_or_above, triangles, triangles.T)
-    lower_right = jnp.where(below, triangles, triangles.T)
-    lower_right = jnp.where(index[:, None] == index[None, :], diagonal[None, :], lower_right)
-    return jnp.concatenate([
-        jnp.concatenate([upper_left, upper_right], axis=1),
-        jnp.concatenate([upper_right.T, lower_right], axis=1),
-    ], axis=0)
-
-
 def on_device(species_field, start_block):
     fibres = lax.all_to_all(species_field, "fibre", split_axis=1, concat_axis=0, tiled=True)
     total_columns = fibres.shape[1] * lax.axis_size("fibre") * lax.axis_size("group")
     fibres, mode_basis = lax.optimization_barrier((fibres, orthonormal(start_block)))
     local_gram = jnp.dot(fibres, fibres.T, precision=product_precision) / total_columns
-    gram_matrix = unpack_symmetric(all_reduce(pack_symmetric(local_gram)))
-    mode_basis = subspace_iteration(gram_matrix, mode_basis)
+    packed_gram = all_reduce(pack_symmetric(local_gram))
+    mode_basis = subspace_iteration(packed_gram, mode_basis)
     core_tensor = jnp.dot(mode_basis.T, fibres, precision=product_precision)
     return (mode_basis, core_tensor)
 

time: 224 us -> 221 us (0.987)
  other arithmetic: 3.21 us -> 0.19 us
  transfers between devices with their start and end apart: 1 -> 1, of which waited for: 1 -> 1; matrix products, arithmetic and copies ran while one was open for 0% -> 0% of each run, Pallas kernels for 3% -> 4%
where the time goes in v9:
time: 221 us; the launch traced here: 220 us
  waiting for transfers between devices  90 us (41%)
  blocking collectives  68.7 us (31%)
  Pallas kernels  30.8 us (14%)
  starting transfers between devices  16.9 us (8%)
  local copies, waits for them, and re-layouts  8.26 us (4%)
  matrix products  4.35 us (2%)
    all_to_all x1, waiting for transfers between devices, on_device(): lax.all_to_all(species_field, 'fibre', split_axis=1, concat_axis=0, tiled...  90 us
    all_to_all x4, blocking collectives, exchange(): return lax.all_to_all(blocks, axis, 0, 0, tiled=True)  68.7 us
    pallas_call x1, Pallas kernels, subspace_iteration(): pl.pallas_call(iterate_kernel, out_shape=jax.ShapeDtypeStruct(mode_basis....  23.1 us
    all_to_all x1, starting transfers between devices, on_device(): lax.all_to_all(species_field, 'fibre', split_axis=1, concat_axis=0, tiled...  16.9 us
    pallas_call x1, Pallas kernels, orthonormal(): pl.pallas_call(orthonormal_kernel, out_shape=jax.ShapeDtypeStruct(matrix....  7.72 us
  transfers between devices with their start and end apart: 1, of which 1 were waited for; matrix products, arithmetic and copies ran while one was open for 0% of the time, Pallas kernels for 4%

profile of v9, /device:TPU:1, one launch (start us, length us, event | category | flops | bytes accessed | tf_op | source)
XLA Modules:
  0.0 220.0 jit_solution(1334206710975430659)
XLA Ops:
  0.6 3.2 %copy.24 = f32[2,32,8,1024]{3,2,0,1:T(8,128)} copy(f32[2,32,8,1024]{3,2,1,0:T(8,128)} %bitcast.17) | data formatting | bytes 4194304 | tf_op jit(solution)/shard_map/all_to_all | solution.py:134
  3.8 0.0 copy-start.1
  3.8 16.9 %all-to-all-start = ((f32[16,32,1024]{2,0,1:T(8,128)}), f32[16,32,1024]{2,0,1:T(8,128)S(1)}, u32[]{:S(2)}, u32[]{:S(2)}) async-start(f32[16,32,1024]{2,0,1:T(8,128)} %bitcast.16), calls=%async_computation | async-start | bytes 4194304 | tf_op jit(solution)/shard_map/all_to_all | solution.py:134
  20.7 0.0 copy-done.1
  20.7 0.8 copy.18.block_ref
  21.6 7.7 %shard_map.41.basis_ref = f32[512,64]{1,0:T(8,128)} custom-call(f32[512,64]{1,0:T(8,128)} %copy.18.block_ref), custom_call_target="tpu_custom_call" | custom-call | tf_op jit(solution)/shard_map/pallas_call | solution.py:77
  29.3 90.0 %all-to-all-done = f32[16,32,1024]{2,0,1:T(8,128)S(1)} async-done(((f32[16,32,1024]{2,0,1:T(8,128)}), f32[16,32,1024]{2,0,1:T(8,128)S(1)}, u32[]{:S(2)}, u32[]{:S(2)}) %all-to-all-start) | async-done | bytes 2097184 | tf_op jit(solution)/shard_map/all_to_all | solution.py:134
  119.3 1.8 convolution_multiply_fusion
  121.2 0.1 slice_select_fusion
  121.2 2.3 %gather_fusion = f32[256]{0:T(256)S(1)} fusion(f32[256,256]{1,0:T(8,128)S(1)} %get-tuple-element.20, s32[256]{0:T(256)S(1)} %bitcast.15), kind=kCustom, calls=%fused_computation | custom fusion | bytes 4096 | tf_op jit(solution)/shard_map/jit(diagonal)/cond/branch_0_fun/gather | solution.py:129
  123.6 0.1 reshape.21
  123.7 18.1 %all_to_all.39 = f32[16,33,256]{2,1,0:T(8,128)S(1)} all-to-all(f32[16,33,256]{2,1,0:T(8,128)S(1)} %reshape.21), channel_id=1, replica_groups=mesh['fibre'=32,'group'=16] {'group'}, dimensions={0} | all-to-all | bytes 1081344 | tf_op jit(solution)/shard_map/all_to_all | solution.py:93
  141.9 19.7 %all_to_all.40 = f32[32,2,256]{2,1,0:T(2,128)S(1)} all-to-all(f32[32,2,256]{2,1,0:T(2,128)S(1)} %reshape.22), channel_id=1, replica_groups=mesh['fibre'=32,'group'=16] {'fibre'}, dimensions={0} | all-to-all | bytes 131072 | tf_op jit(solution)/shard_map/all_to_all | solution.py:93
  161.7 17.3 %all_to_all.41 = f32[32,2,256]{2,1,0:T(2,128)S(1)} all-to-all(f32[32,2,256]{2,1,0:T(2,128)S(1)} %broadcast_in_dim.11), channel_id=1, replica_groups=mesh['fibre'=32,'group'=16] {'fibre'}, dimensions={0} | all-to-all | bytes 131072 | tf_op jit(solution)/shard_map/all_to_all | solution.py:93
  179.1 13.7 %all_to_all.42 = f32[16,33,256]{2,1,0:T(8,128)S(1)} all-to-all(f32[16,33,256]{2,1,0:T(8,128)S(1)} %broadcast_in_dim.12), channel_id=1, replica_groups=mesh['fibre'=32,'group'=16] {'group'}, dimensions={0} | all-to-all | bytes 1081344 | tf_op jit(solution)/shard_map/all_to_all | solution.py:93
  192.7 0.9 reshape.24.packed_ref
  193.6 23.1 %shard_map.42 = f32[512,64]{1,0:T(8,128)} custom-call(f32[528,256]{1,0:T(8,128)} %reshape.24.packed_ref, f32[512,64]{1,0:T(8,128)} %shard_map.41.basis_ref), custom_call_target="tpu_custom_call" | custom-call | tf_op jit(solution)/shard_map/pallas_call | solution.py:85
  216.7 0.0 copy-start
  216.7 2.5 %fusion = f32[64,1024]{1,0:T(8,128)} fusion(f32[512,64]{1,0:T(8,128)} %shard_map.42, f32[512,1024]{1,0:T(8,128)S(1)} %bitcast.14), kind=kOutput, calls=%fused_computation.9 | convolution fusion | flops 201326592 | bytes 2490368 | tf_op jit(solution)/shard_map/dot_general | solution.py:140
  219.2 0.0 copy-done
  219.2 0.8 copy.20
  (10 shorter events, 0.3 us)
Async XLA Ops:
  3.8 16.9 %copy-start.1 = (f32[512,64]{0,1:T(8,128)S(1)}, f32[512,64]{0,1:T(8,128)}, u32[]{:S(2)}) copy-start(f32[512,64]{0,1:T(8,128)} %param.3) | copy-start | bytes 393220
  3.8 115.5 %all-to-all-start = ((f32[16,32,1024]{2,0,1:T(8,128)}), f32[16,32,1024]{2,0,1:T(8,128)S(1)}, u32[]{:S(2)}, u32[]{:S(2)}) async-start(f32[16,32,1024]{2,0,1:T(8,128)} %bitcast.16), calls=%async_computation | async-start | bytes 4194304 | tf_op jit(solution)/shard_map/all_to_all | solution.py:134
  216.7 2.5 %copy-start = (f32[512,64]{1,0:T(8,128)S(1)}, f32[512,64]{1,0:T(8,128)}, u32[]{:S(2)}) copy-start(f32[512,64]{1,0:T(8,128)} %shard_map.42) | copy-start | bytes 393220

commit v10 on v9

--- a/solution.py
+++ b/solution.py
@@ -130,8 +130,35 @@
     return jnp.concatenate([triangles, upper_right, diagonal], axis=0)
 
 
+def chunk_copy_kernel(field_ref, chunks_ref, semaphores):
+    parts, width = chunks_ref.shape[0], chunks_ref.shape[2]
+    copies = [
+        pltpu.make_async_copy(field_ref.at[:, part * width:(part + 1) * width],
+                              chunks_ref.at[part], semaphores.at[part])
+        for part in range(parts)
+    ]
+    for copy in copies:
+        copy.start()
+    for copy in copies:
+        copy.wait()
+
+
+def column_chunks(field, parts):
+    rows, columns = field.shape
+    return pl.pallas_call(
+        chunk_copy_kernel,
+        out_shape=jax.ShapeDtypeStruct((parts, rows, columns // parts), field.dtype),
+        in_specs=[pl.BlockSpec(memory_space=pl.ANY)],
+        out_specs=pl.BlockSpec(memory_space=pl.ANY),
+        scratch_shapes=[pltpu.SemaphoreType.DMA((parts,))],
+    )(field)
+
+
 def on_device(species_field, start_block):
-    fibres = lax.all_to_all(species_field, "fibre", split_axis=1, concat_axis=0, tiled=True)
+    parts = lax.axis_size("fibre")
+    chunks = column_chunks(species_field, parts)
+    fibres = lax.all_to_all(chunks, "fibre", 0, 0, tiled=True)
+    fibres = fibres.reshape(parts * species_field.shape[0], -1)
     total_columns = fibres.shape[1] * lax.axis_size("fibre") * lax.axis_size("group")
     fibres, mode_basis = lax.optimization_barrier((fibres, orthonormal(start_block)))
     local_gram = jnp.dot(fibres, fibres.T, precision=product_precision) / total_columns

time: 221 us -> 283 us (1.28)
  Pallas kernels: 30.8 us -> 95.7 us
  local copies, waits for them, and re-layouts: 8.26 us -> 5.07 us
    pallas_call x0 -> x1, Pallas kernels: none -> 64.9 us  [column_chunks(): pl.pallas_call(chunk_copy_kernel, out_shape=jax.ShapeDtypeStruct((parts,...]
    all_to_all x1 -> x0, local copies, waits for them, and re-layouts: 3.19 us -> none  [on_device(): lax.all_to_all(species_field, 'fibre', split_axis=1, concat_axis=0, tiled...]
  transfers between devices with their start and end apart: 1 -> 1, of which waited for: 1 -> 1; matrix products, arithmetic and copies ran while one was open for 0% -> 0% of each run, Pallas kernels for 4% -> 3%
where the time goes in v10:
time: 283 us; the launch traced here: 282 us
  Pallas kernels  95.7 us (34%)
  waiting for transfers between devices  90 us (32%)
  blocking collectives  68.7 us (24%)
  starting transfers between devices  16.9 us (6%)
  local copies, waits for them, and re-layouts  5.07 us (2%)
  matrix products  4.34 us (2%)
    all_to_all x1, waiting for transfers between devices, on_device(): fibres = lax.all_to_all(chunks, 'fibre', 0, 0, tiled=True)  90 us
    all_to_all x4, blocking collectives, exchange(): return lax.all_to_all(blocks, axis, 0, 0, tiled=True)  68.7 us
    pallas_call x1, Pallas kernels, column_chunks(): pl.pallas_call(chunk_copy_kernel, out_shape=jax.ShapeDtypeStruct((parts,...  64.9 us
    pallas_call x1, Pallas kernels, subspace_iteration(): pl.pallas_call(iterate_kernel, out_shape=jax.ShapeDtypeStruct(mode_basis....  23.1 us
    all_to_all x1, starting transfers between devices, on_device(): fibres = lax.all_to_all(chunks, 'fibre', 0, 0, tiled=True)  16.9 us
    pallas_call x1, Pallas kernels, orthonormal(): pl.pallas_call(orthonormal_kernel, out_shape=jax.ShapeDtypeStruct(matrix....  7.72 us
  transfers between devices with their start and end apart: 1, of which 1 were waited for; matrix products, arithmetic and copies ran while one was open for 0% of the time, Pallas kernels for 3%

profile of v10, /device:TPU:1, one launch (start us, length us, event | category | flops | bytes accessed | tf_op | source)
XLA Modules:
  0.0 281.8 jit_solution(13145476851901137392)
XLA Ops:
  0.6 64.9 %shard_map.41 = f32[32,16,1024]{2,1,0:T(8,128)} custom-call(f32[16,32768]{1,0:T(8,128)} %field_ref.1), custom_call_target="tpu_custom_call" | custom-call | tf_op jit(solution)/shard_map/pallas_call | solution.py:148
  65.6 0.0 copy-start.1
  65.6 16.9 %all-to-all-start = ((f32[32,16,1024]{2,1,0:T(8,128)}), f32[32,16,1024]{2,1,0:T(8,128)S(1)}, u32[]{:S(2)}, u32[]{:S(2)}) async-start(f32[32,16,1024]{2,1,0:T(8,128)} %shard_map.41), calls=%async_computation | async-start | bytes 4194304 | tf_op jit(solution)/shard_map/all_to_all | solution.py:160
  82.5 0.0 copy-done.1
  82.5 0.8 copy.10.block_ref
  83.3 7.7 %shard_map.42.basis_ref = f32[512,64]{1,0:T(8,128)} custom-call(f32[512,64]{1,0:T(8,128)} %copy.10.block_ref), custom_call_target="tpu_custom_call" | custom-call | tf_op jit(solution)/shard_map/pallas_call | solution.py:77
  91.0 90.0 %all-to-all-done = f32[32,16,1024]{2,1,0:T(8,128)S(1)} async-done(((f32[32,16,1024]{2,1,0:T(8,128)}), f32[32,16,1024]{2,1,0:T(8,128)S(1)}, u32[]{:S(2)}, u32[]{:S(2)}) %all-to-all-start) | async-done | bytes 2097184 | tf_op jit(solution)/shard_map/all_to_all | solution.py:160
  181.1 1.8 convolution_multiply_fusion
  182.9 0.1 slice_select_fusion
  183.0 2.3 gather_fusion
  185.4 0.1 reshape.22
  185.5 18.1 %all_to_all.25 = f32[16,33,256]{2,1,0:T(8,128)S(1)} all-to-all(f32[16,33,256]{2,1,0:T(8,128)S(1)} %reshape.22), channel_id=1, replica_groups=mesh['fibre'=32,'group'=16] {'group'}, dimensions={0} | all-to-all | bytes 1081344 | tf_op jit(solution)/shard_map/all_to_all | solution.py:93
  203.7 19.7 %all_to_all.26 = f32[32,2,256]{2,1,0:T(2,128)S(1)} all-to-all(f32[32,2,256]{2,1,0:T(2,128)S(1)} %reshape.23), channel_id=1, replica_groups=mesh['fibre'=32,'group'=16] {'fibre'}, dimensions={0} | all-to-all | bytes 131072 | tf_op jit(solution)/shard_map/all_to_all | solution.py:93
  223.4 17.3 %all_to_all.27 = f32[32,2,256]{2,1,0:T(2,128)S(1)} all-to-all(f32[32,2,256]{2,1,0:T(2,128)S(1)} %broadcast_in_dim.11), channel_id=1, replica_groups=mesh['fibre'=32,'group'=16] {'fibre'}, dimensions={0} | all-to-all | bytes 131072 | tf_op jit(solution)/shard_map/all_to_all | solution.py:93
  240.8 13.7 %all_to_all.28 = f32[16,33,256]{2,1,0:T(8,128)S(1)} all-to-all(f32[16,33,256]{2,1,0:T(8,128)S(1)} %broadcast_in_dim.12), channel_id=1, replica_groups=mesh['fibre'=32,'group'=16] {'group'}, dimensions={0} | all-to-all | bytes 1081344 | tf_op jit(solution)/shard_map/all_to_all | solution.py:93
  254.5 0.9 reshape.25.packed_ref
  255.4 23.1 %shard_map.43 = f32[512,64]{1,0:T(8,128)} custom-call(f32[528,256]{1,0:T(8,128)} %reshape.25.packed_ref, f32[512,64]{1,0:T(8,128)} %shard_map.42.basis_ref), custom_call_target="tpu_custom_call" | custom-call | tf_op jit(solution)/shard_map/pallas_call | solution.py:85
  278.5 0.0 copy-start
  278.5 2.5 fusion
  281.0 0.0 copy-done
  281.0 0.8 copy.12
  (10 shorter events, 0.3 us)
Async XLA Ops:
  65.6 16.9 %copy-start.1 = (f32[512,64]{0,1:T(8,128)S(1)}, f32[512,64]{0,1:T(8,128)}, u32[]{:S(2)}) copy-start(f32[512,64]{0,1:T(8,128)} %param.3) | copy-start | bytes 393220
  65.6 115.5 %all-to-all-start = ((f32[32,16,1024]{2,1,0:T(8,128)}), f32[32,16,1024]{2,1,0:T(8,128)S(1)}, u32[]{:S(2)}, u32[]{:S(2)}) async-start(f32[32,16,1024]{2,1,0:T(8,128)} %shard_map.41), calls=%async_computation | async-start | bytes 4194304 | tf_op jit(solution)/shard_map/all_to_all | solution.py:160
  278.5 2.5 copy-start

commit v11 on v9

--- a/solution.py
+++ b/solution.py
@@ -126,7 +126,8 @@
     index = jnp.arange(half)
     on_or_above = index[:, None] <= index[None, :]
     triangles = jnp.where(on_or_above, upper_left, lower_right)
-    diagonal = jnp.diagonal(lower_right)[None, :]
+    on_diagonal = index[:, None] == index[None, :]
+    diagonal = jnp.sum(jnp.where(on_diagonal, lower_right, 0.0), axis=0, keepdims=True)
     return jnp.concatenate([triangles, upper_right, diagonal], axis=0)
 
 

time: 221 us -> 219 us (level)
  local copies, waits for them, and re-layouts: 8.26 us -> 5.92 us
    gather x1 -> x0, local copies, waits for them, and re-layouts: 2.34 us -> none  [pack_symmetric(): diagonal = jnp.diagonal(lower_right)[None, :]]
where the time goes in v11:
time: 219 us; the launch traced here: 218 us
  waiting for transfers between devices  90 us (41%)
  blocking collectives  68.7 us (31%)
  Pallas kernels  30.8 us (14%)
  starting transfers between devices  16.9 us (8%)
  local copies, waits for them, and re-layouts  5.92 us (3%)
  matrix products  4.35 us (2%)
    all_to_all x1, waiting for transfers between devices, on_device(): lax.all_to_all(species_field, 'fibre', split_axis=1, concat_axis=0, tiled...  90 us
    all_to_all x4, blocking collectives, exchange(): return lax.all_to_all(blocks, axis, 0, 0, tiled=True)  68.7 us
    pallas_call x1, Pallas kernels, subspace_iteration(): pl.pallas_call(iterate_kernel, out_shape=jax.ShapeDtypeStruct(mode_basis....  23.1 us
    all_to_all x1, starting transfers between devices, on_device(): lax.all_to_all(species_field, 'fibre', split_axis=1, concat_axis=0, tiled...  16.9 us
    pallas_call x1, Pallas kernels, orthonormal(): pl.pallas_call(orthonormal_kernel, out_shape=jax.ShapeDtypeStruct(matrix....  7.72 us
  transfers between devices with their start and end apart: 1, of which 1 were waited for; matrix products, arithmetic and copies ran while one was open for 0% of the time, Pallas kernels for 4%

profile of v11, /device:TPU:1, one launch (start us, length us, event | category | flops | bytes accessed | tf_op | source)
XLA Modules:
  0.0 217.7 jit_solution(12195696895553359148)
XLA Ops:
  0.6 3.2 %copy.24 = f32[2,32,8,1024]{3,2,0,1:T(8,128)} copy(f32[2,32,8,1024]{3,2,1,0:T(8,128)} %bitcast.15) | data formatting | bytes 4194304 | tf_op jit(solution)/shard_map/all_to_all | solution.py:135
  3.8 0.0 copy-start.1
  3.8 16.9 %all-to-all-start = ((f32[16,32,1024]{2,0,1:T(8,128)}), f32[16,32,1024]{2,0,1:T(8,128)S(1)}, u32[]{:S(2)}, u32[]{:S(2)}) async-start(f32[16,32,1024]{2,0,1:T(8,128)} %bitcast.14), calls=%async_computation | async-start | bytes 4194304 | tf_op jit(solution)/shard_map/all_to_all | solution.py:135
  20.7 0.0 copy-done.1
  20.7 0.8 copy.18.block_ref
  21.6 7.7 %shard_map.41.basis_ref = f32[512,64]{1,0:T(8,128)} custom-call(f32[512,64]{1,0:T(8,128)} %copy.18.block_ref), custom_call_target="tpu_custom_call" | custom-call | tf_op jit(solution)/shard_map/pallas_call | solution.py:77
  29.3 90.0 %all-to-all-done = f32[16,32,1024]{2,0,1:T(8,128)S(1)} async-done(((f32[16,32,1024]{2,0,1:T(8,128)}), f32[16,32,1024]{2,0,1:T(8,128)S(1)}, u32[]{:S(2)}, u32[]{:S(2)}) %all-to-all-start) | async-done | bytes 2097184 | tf_op jit(solution)/shard_map/all_to_all | solution.py:135
  119.3 1.8 convolution_multiply_fusion
  121.2 0.1 slice_select_fusion
  121.3 0.1 reshape.21
  121.4 18.1 %all_to_all.39 = f32[16,33,256]{2,1,0:T(8,128)S(1)} all-to-all(f32[16,33,256]{2,1,0:T(8,128)S(1)} %reshape.21), channel_id=1, replica_groups=mesh['fibre'=32,'group'=16] {'group'}, dimensions={0} | all-to-all | bytes 1081344 | tf_op jit(solution)/shard_map/all_to_all | solution.py:93
  139.6 19.7 %all_to_all.40 = f32[32,2,256]{2,1,0:T(2,128)S(1)} all-to-all(f32[32,2,256]{2,1,0:T(2,128)S(1)} %reshape.22), channel_id=1, replica_groups=mesh['fibre'=32,'group'=16] {'fibre'}, dimensions={0} | all-to-all | bytes 131072 | tf_op jit(solution)/shard_map/all_to_all | solution.py:93
  159.3 17.3 %all_to_all.41 = f32[32,2,256]{2,1,0:T(2,128)S(1)} all-to-all(f32[32,2,256]{2,1,0:T(2,128)S(1)} %broadcast_in_dim.12), channel_id=1, replica_groups=mesh['fibre'=32,'group'=16] {'fibre'}, dimensions={0} | all-to-all | bytes 131072 | tf_op jit(solution)/shard_map/all_to_all | solution.py:93
  176.7 13.7 %all_to_all.42 = f32[16,33,256]{2,1,0:T(8,128)S(1)} all-to-all(f32[16,33,256]{2,1,0:T(8,128)S(1)} %broadcast_in_dim.13), channel_id=1, replica_groups=mesh['fibre'=32,'group'=16] {'group'}, dimensions={0} | all-to-all | bytes 1081344 | tf_op jit(solution)/shard_map/all_to_all | solution.py:93
  190.4 0.9 reshape.24.packed_ref
  191.3 23.1 %shard_map.42 = f32[512,64]{1,0:T(8,128)} custom-call(f32[528,256]{1,0:T(8,128)} %reshape.24.packed_ref, f32[512,64]{1,0:T(8,128)} %shard_map.41.basis_ref), custom_call_target="tpu_custom_call" | custom-call | tf_op jit(solution)/shard_map/pallas_call | solution.py:85
  214.4 0.0 copy-start
  214.4 2.5 %fusion = f32[64,1024]{1,0:T(8,128)} fusion(f32[512,64]{1,0:T(8,128)} %shard_map.42, f32[512,1024]{1,0:T(8,128)S(1)} %bitcast.13), kind=kOutput, calls=%fused_computation.9 | convolution fusion | flops 201326592 | bytes 2490368 | tf_op jit(solution)/shard_map/dot_general | solution.py:141
  216.9 0.0 copy-done
  216.9 0.8 copy.20
  (9 shorter events, 0.3 us)
Async XLA Ops:
  3.8 16.9 %copy-start.1 = (f32[512,64]{0,1:T(8,128)S(1)}, f32[512,64]{0,1:T(8,128)}, u32[]{:S(2)}) copy-start(f32[512,64]{0,1:T(8,128)} %param.3) | copy-start | bytes 393220
  3.8 115.5 %all-to-all-start = ((f32[16,32,1024]{2,0,1:T(8,128)}), f32[16,32,1024]{2,0,1:T(8,128)S(1)}, u32[]{:S(2)}, u32[]{:S(2)}) async-start(f32[16,32,1024]{2,0,1:T(8,128)} %bitcast.14), calls=%async_computation | async-start | bytes 4194304 | tf_op jit(solution)/shard_map/all_to_all | solution.py:135
  214.4 2.5 %copy-start = (f32[512,64]{1,0:T(8,128)S(1)}, f32[512,64]{1,0:T(8,128)}, u32[]{:S(2)}) copy-start(f32[512,64]{1,0:T(8,128)} %shard_map.42) | copy-start | bytes 393220

commit v12 on v11

--- a/solution.py
+++ b/solution.py
@@ -66,11 +66,18 @@
     gram_ref[0:half, half:] = upper_right
     gram_ref[half:, 0:half] = upper_right.T
     basis = basis_ref[...]
-    for iteration in range(ITERS):
+    for iteration in range(ITERS - 1):
         product = jnp.dot(gram_ref[...], basis, precision=product_precision,
                           preferred_element_type=jnp.float32)
         basis = orthonormal_in_kernel(product)
-    out_ref[...] = basis
+    product = jnp.dot(gram_ref[...], basis, precision=product_precision,
+                      preferred_element_type=jnp.float32)
+    inner_gram = jnp.dot(product.T, product, precision=highest_precision,
+                         preferred_element_type=jnp.float32)
+    out_ref[...] = lax.dot_general(
+        inverse_cholesky(inner_gram), product, (((1,), (1,)), ((), ())),
+        precision=highest_precision, preferred_element_type=jnp.float32,
+    )
 
 
 def orthonormal(matrix):
@@ -84,7 +91,7 @@
     size = 2 * packed_gram.shape[1]
     return pl.pallas_call(
         iterate_kernel,
-        out_shape=jax.ShapeDtypeStruct(mode_basis.shape, jnp.float32),
+        out_shape=jax.ShapeDtypeStruct(mode_basis.shape[::-1], jnp.float32),
         scratch_shapes=[pltpu.VMEM((size, size), jnp.float32)],
     )(packed_gram, mode_basis)
 
@@ -137,9 +144,9 @@
     fibres, mode_basis = lax.optimization_barrier((fibres, orthonormal(start_block)))
     local_gram = jnp.dot(fibres, fibres.T, precision=product_precision) / total_columns
     packed_gram = all_reduce(pack_symmetric(local_gram))
-    mode_basis = subspace_iteration(packed_gram, mode_basis)
-    core_tensor = jnp.dot(mode_basis.T, fibres, precision=product_precision)
-    return (mode_basis, core_tensor)
+    basis_rows = subspace_iteration(packed_gram, mode_basis)
+    core_tensor = jnp.dot(basis_rows, fibres, precision=product_precision)
+    return (basis_rows.T, core_tensor)
 
 
 def solution(mesh):

time: 219 us -> 218 us (level)
  no operation moved by 1% of the time
where the time goes in v12:
time: 218 us; the launch traced here: 217 us
  waiting for transfers between devices  90 us (41%)
  blocking collectives  68.7 us (32%)
  Pallas kernels  30.7 us (14%)
  starting transfers between devices  16.9 us (8%)
  local copies, waits for them, and re-layouts  5.14 us (2%)
  matrix products  4.21 us (2%)
    all_to_all x1, waiting for transfers between devices, on_device(): lax.all_to_all(species_field, 'fibre', split_axis=1, concat_axis=0, tiled...  90 us
    all_to_all x4, blocking collectives, exchange(): return lax.all_to_all(blocks, axis, 0, 0, tiled=True)  68.7 us
    pallas_call x1, Pallas kernels, subspace_iteration(): pl.pallas_call(iterate_kernel, out_shape=jax.ShapeDtypeStruct(mode_basis....  23 us
    all_to_all x1, starting transfers between devices, on_device(): lax.all_to_all(species_field, 'fibre', split_axis=1, concat_axis=0, tiled...  16.9 us
    pallas_call x1, Pallas kernels, orthonormal(): pl.pallas_call(orthonormal_kernel, out_shape=jax.ShapeDtypeStruct(matrix....  7.71 us
  transfers between devices with their start and end apart: 1, of which 1 were waited for; matrix products, arithmetic and copies ran while one was open for 0% of the time, Pallas kernels for 4%

profile of v12, /device:TPU:1, one launch (start us, length us, event | category | flops | bytes accessed | tf_op | source)
XLA Modules:
  0.0 216.7 jit_solution(17141208849820243252)
XLA Ops:
  0.6 3.2 %copy.18 = f32[2,32,8,1024]{3,2,0,1:T(8,128)} copy(f32[2,32,8,1024]{3,2,1,0:T(8,128)} %bitcast.16) | data formatting | bytes 4194304 | tf_op jit(solution)/shard_map/all_to_all | solution.py:142
  3.8 0.0 copy-start
  3.8 16.9 %all-to-all-start = ((f32[16,32,1024]{2,0,1:T(8,128)}), f32[16,32,1024]{2,0,1:T(8,128)S(1)}, u32[]{:S(2)}, u32[]{:S(2)}) async-start(f32[16,32,1024]{2,0,1:T(8,128)} %bitcast.15), calls=%async_computation | async-start | bytes 4194304 | tf_op jit(solution)/shard_map/all_to_all | solution.py:142
  20.7 0.0 copy-done
  20.7 0.8 copy.13.block_ref
  21.6 7.7 %shard_map.41.basis_ref = f32[512,64]{1,0:T(8,128)} custom-call(f32[512,64]{1,0:T(8,128)} %copy.13.block_ref), custom_call_target="tpu_custom_call" | custom-call | tf_op jit(solution)/shard_map/pallas_call | solution.py:84
  29.3 90.0 %all-to-all-done = f32[16,32,1024]{2,0,1:T(8,128)S(1)} async-done(((f32[16,32,1024]{2,0,1:T(8,128)}), f32[16,32,1024]{2,0,1:T(8,128)S(1)}, u32[]{:S(2)}, u32[]{:S(2)}) %all-to-all-start) | async-done | bytes 2097184 | tf_op jit(solution)/shard_map/all_to_all | solution.py:142
  119.3 1.8 convolution_multiply_fusion
  121.2 0.1 slice_select_fusion
  121.3 0.1 reshape.21
  121.4 18.1 %all_to_all.39 = f32[16,33,256]{2,1,0:T(8,128)S(1)} all-to-all(f32[16,33,256]{2,1,0:T(8,128)S(1)} %reshape.21), channel_id=1, replica_groups=mesh['fibre'=32,'group'=16] {'group'}, dimensions={0} | all-to-all | bytes 1081344 | tf_op jit(solution)/shard_map/all_to_all | solution.py:100
  139.6 19.7 %all_to_all.40 = f32[32,2,256]{2,1,0:T(2,128)S(1)} all-to-all(f32[32,2,256]{2,1,0:T(2,128)S(1)} %reshape.22), channel_id=1, replica_groups=mesh['fibre'=32,'group'=16] {'fibre'}, dimensions={0} | all-to-all | bytes 131072 | tf_op jit(solution)/shard_map/all_to_all | solution.py:100
  159.3 17.3 %all_to_all.41 = f32[32,2,256]{2,1,0:T(2,128)S(1)} all-to-all(f32[32,2,256]{2,1,0:T(2,128)S(1)} %broadcast_in_dim.12), channel_id=1, replica_groups=mesh['fibre'=32,'group'=16] {'fibre'}, dimensions={0} | all-to-all | bytes 131072 | tf_op jit(solution)/shard_map/all_to_all | solution.py:100
  176.7 13.7 %all_to_all.42 = f32[16,33,256]{2,1,0:T(8,128)S(1)} all-to-all(f32[16,33,256]{2,1,0:T(8,128)S(1)} %broadcast_in_dim.13), channel_id=1, replica_groups=mesh['fibre'=32,'group'=16] {'group'}, dimensions={0} | all-to-all | bytes 1081344 | tf_op jit(solution)/shard_map/all_to_all | solution.py:100
  190.4 0.9 reshape.24.packed_ref
  191.3 23.0 %shard_map.42 = f32[64,512]{1,0:T(8,128)} custom-call(f32[528,256]{1,0:T(8,128)} %reshape.24.packed_ref, f32[512,64]{1,0:T(8,128)} %shard_map.41.basis_ref), custom_call_target="tpu_custom_call" | custom-call | tf_op jit(solution)/shard_map/pallas_call | solution.py:92
  214.3 2.4 %fusion = f32[64,1024]{1,0:T(8,128)} fusion(f32[64,512]{1,0:T(8,128)} %shard_map.42, f32[512,1024]{1,0:T(8,128)S(1)} %bitcast.14), kind=kOutput, calls=%fused_computation.9 | convolution fusion | flops 201326592 | bytes 2490368 | tf_op jit(solution)/shard_map/dot_general | solution.py:148
  (9 shorter events, 0.3 us)
Async XLA Ops:
  3.8 16.9 %copy-start = (f32[512,64]{0,1:T(8,128)S(1)}, f32[512,64]{0,1:T(8,128)}, u32[]{:S(2)}) copy-start(f32[512,64]{0,1:T(8,128)} %param.3) | copy-start | bytes 393220
  3.8 115.5 %all-to-all-start = ((f32[16,32,1024]{2,0,1:T(8,128)}), f32[16,32,1024]{2,0,1:T(8,128)S(1)}, u32[]{:S(2)}, u32[]{:S(2)}) async-start(f32[16,32,1024]{2,0,1:T(8,128)} %bitcast.15), calls=%async_computation | async-start | bytes 4194304 | tf_op jit(solution)/shard_map/all_to_all | solution.py:142

commit v13 on v12

--- a/solution.py
+++ b/solution.py
@@ -118,7 +118,8 @@
 
 def all_reduce(matrix):
     groups, fibres = lax.axis_size("group"), lax.axis_size("fibre")
-    rows = pad_rows(matrix, -(-matrix.shape[0] // groups) * groups)
+    chunk = -(-matrix.shape[0] // groups)
+    rows = pad_rows(matrix, -(-chunk // 8) * 8 * groups)
     rows = reduce_scatter(rows, "group")
     chunk = rows.shape[0]
     rows = pad_rows(rows, -(-chunk // fibres) * fibres)

time: 218 us -> 217 us (level)
  no operation moved by 1% of the time
where the time goes in v13:
time: 217 us
  waiting for transfers between devices  90 us (41%)
  blocking collectives  69.8 us (32%)
  Pallas kernels  30.8 us (14%)
  starting transfers between devices  16.9 us (8%)
  matrix products  4.21 us (2%)
  local copies, waits for them, and re-layouts  4.18 us (2%)
    all_to_all x1, waiting for transfers between devices, on_device(): lax.all_to_all(species_field, 'fibre', split_axis=1, concat_axis=0, tiled...  90 us
    all_to_all x4, blocking collectives, exchange(): return lax.all_to_all(blocks, axis, 0, 0, tiled=True)  69.8 us
    pallas_call x1, Pallas kernels, subspace_iteration(): pl.pallas_call(iterate_kernel, out_shape=jax.ShapeDtypeStruct(mode_basis....  23.1 us
    all_to_all x1, starting transfers between devices, on_device(): lax.all_to_all(species_field, 'fibre', split_axis=1, concat_axis=0, tiled...  16.9 us
    pallas_call x1, Pallas kernels, orthonormal(): pl.pallas_call(orthonormal_kernel, out_shape=jax.ShapeDtypeStruct(matrix....  7.71 us
  transfers between devices with their start and end apart: 1, of which 1 were waited for; matrix products, arithmetic and copies ran while one was open for 0% of the time, Pallas kernels for 4%

profile of v13, /device:TPU:1, one launch (start us, length us, event | category | flops | bytes accessed | tf_op | source)
XLA Modules:
  0.0 216.7 jit_solution(14675857675899976344)
XLA Ops:
  0.6 3.2 %copy.18 = f32[2,32,8,1024]{3,2,0,1:T(8,128)} copy(f32[2,32,8,1024]{3,2,1,0:T(8,128)} %bitcast.20) | data formatting | bytes 4194304 | tf_op jit(solution)/shard_map/all_to_all | solution.py:143
  3.8 0.0 copy-start
  3.8 16.9 %all-to-all-start = ((f32[16,32,1024]{2,0,1:T(8,128)}), f32[16,32,1024]{2,0,1:T(8,128)S(1)}, u32[]{:S(2)}, u32[]{:S(2)}) async-start(f32[16,32,1024]{2,0,1:T(8,128)} %bitcast.17), calls=%async_computation | async-start | bytes 4194304 | tf_op jit(solution)/shard_map/all_to_all | solution.py:143
  20.7 0.0 copy-done
  20.7 0.8 copy.13.block_ref
  21.6 7.7 %shard_map.41.basis_ref = f32[512,64]{1,0:T(8,128)} custom-call(f32[512,64]{1,0:T(8,128)} %copy.13.block_ref), custom_call_target="tpu_custom_call" | custom-call | tf_op jit(solution)/shard_map/pallas_call | solution.py:84
  29.3 90.0 %all-to-all-done = f32[16,32,1024]{2,0,1:T(8,128)S(1)} async-done(((f32[16,32,1024]{2,0,1:T(8,128)}), f32[16,32,1024]{2,0,1:T(8,128)S(1)}, u32[]{:S(2)}, u32[]{:S(2)}) %all-to-all-start) | async-done | bytes 2097184 | tf_op jit(solution)/shard_map/all_to_all | solution.py:143
  119.3 1.8 convolution_multiply_fusion
  121.2 0.1 slice_select_fusion
  121.3 18.1 %all_to_all.39 = f32[16,40,256]{2,1,0:T(8,128)S(1)} all-to-all(f32[16,40,256]{2,1,0:T(8,128)S(1)} %bitcast.18), channel_id=1, replica_groups=mesh['fibre'=32,'group'=16] {'group'}, dimensions={0} | all-to-all | bytes 1310720 | tf_op jit(solution)/shard_map/all_to_all | solution.py:100
  139.5 19.7 %all_to_all.40 = f32[32,2,256]{2,1,0:T(2,128)S(1)} all-to-all(f32[32,2,256]{2,1,0:T(2,128)S(1)} %reshape.22), channel_id=1, replica_groups=mesh['fibre'=32,'group'=16] {'fibre'}, dimensions={0} | all-to-all | bytes 131072 | tf_op jit(solution)/shard_map/all_to_all | solution.py:100
  159.3 17.3 %all_to_all.41 = f32[32,2,256]{2,1,0:T(2,128)S(1)} all-to-all(f32[32,2,256]{2,1,0:T(2,128)S(1)} %broadcast_in_dim.14), channel_id=1, replica_groups=mesh['fibre'=32,'group'=16] {'fibre'}, dimensions={0} | all-to-all | bytes 131072 | tf_op jit(solution)/shard_map/all_to_all | solution.py:100
  176.6 14.7 %all_to_all.42 = f32[16,40,256]{2,1,0:T(8,128)} all-to-all(f32[16,40,256]{2,1,0:T(8,128)S(1)} %broadcast_in_dim.29), channel_id=1, replica_groups=mesh['fibre'=32,'group'=16] {'group'}, dimensions={0} | all-to-all | bytes 1310720 | tf_op jit(solution)/shard_map/all_to_all | solution.py:100
  191.3 23.1 %shard_map.42 = f32[64,512]{1,0:T(8,128)} custom-call(f32[640,256]{1,0:T(8,128)} %bitcast.19, f32[512,64]{1,0:T(8,128)} %shard_map.41.basis_ref), custom_call_target="tpu_custom_call" | custom-call | tf_op jit(solution)/shard_map/pallas_call | solution.py:92
  214.4 2.4 %fusion = f32[64,1024]{1,0:T(8,128)} fusion(f32[64,512]{1,0:T(8,128)} %shard_map.42, f32[512,1024]{1,0:T(8,128)S(1)} %bitcast.16), kind=kOutput, calls=%fused_computation.9 | convolution fusion | flops 201326592 | bytes 2490368 | tf_op jit(solution)/shard_map/dot_general | solution.py:149
  (9 shorter events, 0.3 us)
Async XLA Ops:
  3.8 16.9 %copy-start = (f32[512,64]{0,1:T(8,128)S(1)}, f32[512,64]{0,1:T(8,128)}, u32[]{:S(2)}) copy-start(f32[512,64]{0,1:T(8,128)} %param.3) | copy-start | bytes 393220
  3.8 115.5 %all-to-all-start = ((f32[16,32,1024]{2,0,1:T(8,128)}), f32[16,32,1024]{2,0,1:T(8,128)S(1)}, u32[]{:S(2)}, u32[]{:S(2)}) async-start(f32[16,32,1024]{2,0,1:T(8,128)} %bitcast.17), calls=%async_computation | async-start | bytes 4194304 | tf_op jit(solution)/shard_map/all_to_all | solution.py:143

commit v14 on v13

--- a/solution.py
+++ b/solution.py
@@ -128,9 +128,12 @@
     return gather(rows, "group")
 
 
-def pack_symmetric(gram):
-    half = gram.shape[0] // 2
-    upper_left, upper_right, lower_right = gram[:half, :half], gram[:half, half:], gram[half:, half:]
+def packed_gram_of(fibres, total_columns):
+    half = fibres.shape[0] // 2
+    top, bottom = fibres[:half], fibres[half:]
+    upper_left = jnp.dot(top, top.T, precision=product_precision) / total_columns
+    upper_right = jnp.dot(top, bottom.T, precision=product_precision) / total_columns
+    lower_right = jnp.dot(bottom, bottom.T, precision=product_precision) / total_columns
     index = jnp.arange(half)
     on_or_above = index[:, None] <= index[None, :]
     triangles = jnp.where(on_or_above, upper_left, lower_right)
@@ -143,8 +146,7 @@
     fibres = lax.all_to_all(species_field, "fibre", split_axis=1, concat_axis=0, tiled=True)
     total_columns = fibres.shape[1] * lax.axis_size("fibre") * lax.axis_size("group")
     fibres, mode_basis = lax.optimization_barrier((fibres, orthonormal(start_block)))
-    local_gram = jnp.dot(fibres, fibres.T, precision=product_precision) / total_columns
-    packed_gram = all_reduce(pack_symmetric(local_gram))
+    packed_gram = all_reduce(packed_gram_of(fibres, total_columns))
     basis_rows = subspace_iteration(packed_gram, mode_basis)
     core_tensor = jnp.dot(basis_rows, fibres, precision=product_precision)
     return (basis_rows.T, core_tensor)

time: 217 us -> 217 us (level)
  no operation moved by 1% of the time
where the time goes in v14:
time: 217 us
  waiting for transfers between devices  90 us (41%)
  blocking collectives  69.7 us (32%)
  Pallas kernels  30.8 us (14%)
  starting transfers between devices  16.9 us (8%)
  matrix products  4.26 us (2%)
  local copies, waits for them, and re-layouts  4.18 us (2%)
    all_to_all x1, waiting for transfers between devices, on_device(): lax.all_to_all(species_field, 'fibre', split_axis=1, concat_axis=0, tiled...  90 us
    all_to_all x4, blocking collectives, exchange(): return lax.all_to_all(blocks, axis, 0, 0, tiled=True)  69.7 us
    pallas_call x1, Pallas kernels, subspace_iteration(): pl.pallas_call(iterate_kernel, out_shape=jax.ShapeDtypeStruct(mode_basis....  23.1 us
    all_to_all x1, starting transfers between devices, on_device(): lax.all_to_all(species_field, 'fibre', split_axis=1, concat_axis=0, tiled...  16.9 us
    pallas_call x1, Pallas kernels, orthonormal(): pl.pallas_call(orthonormal_kernel, out_shape=jax.ShapeDtypeStruct(matrix....  7.71 us
  transfers between devices with their start and end apart: 1, of which 1 were waited for; matrix products, arithmetic and copies ran while one was open for 0% of the time, Pallas kernels for 4%

profile of v14, /device:TPU:1, one launch (start us, length us, event | category | flops | bytes accessed | tf_op | source)
XLA Modules:
  0.0 216.7 jit_solution(4339054899058158648)
XLA Ops:
  0.6 3.2 %copy.18 = f32[2,32,8,1024]{3,2,0,1:T(8,128)} copy(f32[2,32,8,1024]{3,2,1,0:T(8,128)} %bitcast.20) | data formatting | bytes 4194304 | tf_op jit(solution)/shard_map/all_to_all | solution.py:146
  3.8 0.0 copy-start
  3.8 16.9 %all-to-all-start = ((f32[16,32,1024]{2,0,1:T(8,128)}), f32[16,32,1024]{2,0,1:T(8,128)S(1)}, u32[]{:S(2)}, u32[]{:S(2)}) async-start(f32[16,32,1024]{2,0,1:T(8,128)} %bitcast.17), calls=%async_computation | async-start | bytes 4194304 | tf_op jit(solution)/shard_map/all_to_all | solution.py:146
  20.7 0.0 copy-done
  20.7 0.8 copy.13.block_ref
  21.6 7.7 %shard_map.41.basis_ref = f32[512,64]{1,0:T(8,128)} custom-call(f32[512,64]{1,0:T(8,128)} %copy.13.block_ref), custom_call_target="tpu_custom_call" | custom-call | tf_op jit(solution)/shard_map/pallas_call | solution.py:84
  29.3 90.0 %all-to-all-done = f32[16,32,1024]{2,0,1:T(8,128)S(1)} async-done(((f32[16,32,1024]{2,0,1:T(8,128)}), f32[16,32,1024]{2,0,1:T(8,128)S(1)}, u32[]{:S(2)}, u32[]{:S(2)}) %all-to-all-start) | async-done | bytes 2097184 | tf_op jit(solution)/shard_map/all_to_all | solution.py:146
  119.3 0.6 select_reduce_fusion
  120.0 0.6 convolution_multiply_fusion
  120.6 0.6 fusion
  121.3 18.1 %all_to_all.39 = f32[16,40,256]{2,1,0:T(8,128)S(1)} all-to-all(f32[16,40,256]{2,1,0:T(8,128)S(1)} %bitcast.18), channel_id=1, replica_groups=mesh['fibre'=32,'group'=16] {'group'}, dimensions={0} | all-to-all | bytes 1310720 | tf_op jit(solution)/shard_map/all_to_all | solution.py:100
  139.5 19.7 %all_to_all.40 = f32[32,2,256]{2,1,0:T(2,128)S(1)} all-to-all(f32[32,2,256]{2,1,0:T(2,128)S(1)} %reshape.22), channel_id=1, replica_groups=mesh['fibre'=32,'group'=16] {'fibre'}, dimensions={0} | all-to-all | bytes 131072 | tf_op jit(solution)/shard_map/all_to_all | solution.py:100
  159.3 17.3 %all_to_all.41 = f32[32,2,256]{2,1,0:T(2,128)S(1)} all-to-all(f32[32,2,256]{2,1,0:T(2,128)S(1)} %broadcast_in_dim.14), channel_id=1, replica_groups=mesh['fibre'=32,'group'=16] {'fibre'}, dimensions={0} | all-to-all | bytes 131072 | tf_op jit(solution)/shard_map/all_to_all | solution.py:100
  176.6 14.7 %all_to_all.42 = f32[16,40,256]{2,1,0:T(8,128)} all-to-all(f32[16,40,256]{2,1,0:T(8,128)S(1)} %broadcast_in_dim.29), channel_id=1, replica_groups=mesh['fibre'=32,'group'=16] {'group'}, dimensions={0} | all-to-all | bytes 1310720 | tf_op jit(solution)/shard_map/all_to_all | solution.py:100
  191.3 23.1 %shard_map.42 = f32[64,512]{1,0:T(8,128)} custom-call(f32[640,256]{1,0:T(8,128)} %bitcast.19, f32[512,64]{1,0:T(8,128)} %shard_map.41.basis_ref), custom_call_target="tpu_custom_call" | custom-call | tf_op jit(solution)/shard_map/pallas_call | solution.py:92
  214.4 2.4 %fusion.5 = f32[64,1024]{1,0:T(8,128)} fusion(f32[64,512]{1,0:T(8,128)} %shard_map.42, f32[512,1024]{1,0:T(8,128)S(1)} %bitcast.16), kind=kOutput, calls=%fused_computation.15 | convolution fusion | flops 201326592 | bytes 2490368 | tf_op jit(solution)/shard_map/dot_general | solution.py:151
  (9 shorter events, 0.3 us)
Async XLA Ops:
  3.8 16.9 %copy-start = (f32[512,64]{0,1:T(8,128)S(1)}, f32[512,64]{0,1:T(8,128)}, u32[]{:S(2)}) copy-start(f32[512,64]{0,1:T(8,128)} %param.3) | copy-start | bytes 393220
  3.8 115.5 %all-to-all-start = ((f32[16,32,1024]{2,0,1:T(8,128)}), f32[16,32,1024]{2,0,1:T(8,128)S(1)}, u32[]{:S(2)}, u32[]{:S(2)}) async-start(f32[16,32,1024]{2,0,1:T(8,128)} %bitcast.17), calls=%async_computation | async-start | bytes 4194304 | tf_op jit(solution)/shard_map/all_to_all | solution.py:146

commit v15 on v13

--- a/solution.py
+++ b/solution.py
@@ -39,11 +39,11 @@
 
 
 def orthonormal_in_kernel(matrix):
-    inner_gram = jnp.dot(matrix.T, matrix, precision=highest_precision,
+    inner_gram = jnp.dot(matrix.T, matrix, precision=product_precision,
                          preferred_element_type=jnp.float32)
     lower_inverse = inverse_cholesky(inner_gram)
     return lax.dot_general(
-        matrix, lower_inverse, (((1,), (1,)), ((), ())), precision=highest_precision,
+        matrix, lower_inverse, (((1,), (1,)), ((), ())), precision=product_precision,
         preferred_element_type=jnp.float32,
     )
 
@@ -72,11 +72,11 @@
         basis = orthonormal_in_kernel(product)
     product = jnp.dot(gram_ref[...], basis, precision=product_precision,
                       preferred_element_type=jnp.float32)
-    inner_gram = jnp.dot(product.T, product, precision=highest_precision,
+    inner_gram = jnp.dot(product.T, product, precision=product_precision,
                          preferred_element_type=jnp.float32)
     out_ref[...] = lax.dot_general(
         inverse_cholesky(inner_gram), product, (((1,), (1,)), ((), ())),
-        precision=highest_precision, preferred_element_type=jnp.float32,
+        precision=product_precision, preferred_element_type=jnp.float32,
     )
 
 

time: 217 us -> 216 us (level)
  no operation moved by 1% of the time
where the time goes in v15:
time: 216 us
  waiting for transfers between devices  90.2 us (42%)
  blocking collectives  69.8 us (32%)
  Pallas kernels  29.6 us (14%)
  starting transfers between devices  16.9 us (8%)
  matrix products  4.21 us (2%)
  local copies, waits for them, and re-layouts  4.18 us (2%)
    all_to_all x1, waiting for transfers between devices, on_device(): lax.all_to_all(species_field, 'fibre', split_axis=1, concat_axis=0, tiled...  90.2 us
    all_to_all x4, blocking collectives, exchange(): return lax.all_to_all(blocks, axis, 0, 0, tiled=True)  69.8 us
    pallas_call x1, Pallas kernels, subspace_iteration(): pl.pallas_call(iterate_kernel, out_shape=jax.ShapeDtypeStruct(mode_basis....  22 us
    all_to_all x1, starting transfers between devices, on_device(): lax.all_to_all(species_field, 'fibre', split_axis=1, concat_axis=0, tiled...  16.9 us
    pallas_call x1, Pallas kernels, orthonormal(): pl.pallas_call(orthonormal_kernel, out_shape=jax.ShapeDtypeStruct(matrix....  7.58 us
  transfers between devices with their start and end apart: 1, of which 1 were waited for; matrix products, arithmetic and copies ran while one was open for 0% of the time, Pallas kernels for 4%

profile of v15, /device:TPU:1, one launch (start us, length us, event | category | flops | bytes accessed | tf_op | source)
XLA Modules:
  0.0 215.7 jit_solution(14937671110946491850)
XLA Ops:
  0.6 3.2 %copy.18 = f32[2,32,8,1024]{3,2,0,1:T(8,128)} copy(f32[2,32,8,1024]{3,2,1,0:T(8,128)} %bitcast.20) | data formatting | bytes 4194304 | tf_op jit(solution)/shard_map/all_to_all | solution.py:143
  3.8 0.0 copy-start
  3.8 16.9 %all-to-all-start = ((f32[16,32,1024]{2,0,1:T(8,128)}), f32[16,32,1024]{2,0,1:T(8,128)S(1)}, u32[]{:S(2)}, u32[]{:S(2)}) async-start(f32[16,32,1024]{2,0,1:T(8,128)} %bitcast.17), calls=%async_computation | async-start | bytes 4194304 | tf_op jit(solution)/shard_map/all_to_all | solution.py:143
  20.7 0.0 copy-done
  20.7 0.8 copy.13.block_ref
  21.6 7.6 %shard_map.41.basis_ref = f32[512,64]{1,0:T(8,128)} custom-call(f32[512,64]{1,0:T(8,128)} %copy.13.block_ref), custom_call_target="tpu_custom_call" | custom-call | tf_op jit(solution)/shard_map/pallas_call | solution.py:84
  29.1 90.2 %all-to-all-done = f32[16,32,1024]{2,0,1:T(8,128)S(1)} async-done(((f32[16,32,1024]{2,0,1:T(8,128)}), f32[16,32,1024]{2,0,1:T(8,128)S(1)}, u32[]{:S(2)}, u32[]{:S(2)}) %all-to-all-start) | async-done | bytes 2097184 | tf_op jit(solution)/shard_map/all_to_all | solution.py:143
  119.3 1.8 convolution_multiply_fusion
  121.2 0.1 slice_select_fusion
  121.3 18.1 %all_to_all.39 = f32[16,40,256]{2,1,0:T(8,128)S(1)} all-to-all(f32[16,40,256]{2,1,0:T(8,128)S(1)} %bitcast.18), channel_id=1, replica_groups=mesh['fibre'=32,'group'=16] {'group'}, dimensions={0} | all-to-all | bytes 1310720 | tf_op jit(solution)/shard_map/all_to_all | solution.py:100
  139.5 19.7 %all_to_all.40 = f32[32,2,256]{2,1,0:T(2,128)S(1)} all-to-all(f32[32,2,256]{2,1,0:T(2,128)S(1)} %reshape.22), channel_id=1, replica_groups=mesh['fibre'=32,'group'=16] {'fibre'}, dimensions={0} | all-to-all | bytes 131072 | tf_op jit(solution)/shard_map/all_to_all | solution.py:100
  159.3 17.3 %all_to_all.41 = f32[32,2,256]{2,1,0:T(2,128)S(1)} all-to-all(f32[32,2,256]{2,1,0:T(2,128)S(1)} %broadcast_in_dim.14), channel_id=1, replica_groups=mesh['fibre'=32,'group'=16] {'fibre'}, dimensions={0} | all-to-all | bytes 131072 | tf_op jit(solution)/shard_map/all_to_all | solution.py:100
  176.6 14.7 %all_to_all.42 = f32[16,40,256]{2,1,0:T(8,128)} all-to-all(f32[16,40,256]{2,1,0:T(8,128)S(1)} %broadcast_in_dim.29), channel_id=1, replica_groups=mesh['fibre'=32,'group'=16] {'group'}, dimensions={0} | all-to-all | bytes 1310720 | tf_op jit(solution)/shard_map/all_to_all | solution.py:100
  191.3 22.0 %shard_map.42 = f32[64,512]{1,0:T(8,128)} custom-call(f32[640,256]{1,0:T(8,128)} %bitcast.19, f32[512,64]{1,0:T(8,128)} %shard_map.41.basis_ref), custom_call_target="tpu_custom_call" | custom-call | tf_op jit(solution)/shard_map/pallas_call | solution.py:92
  213.3 2.4 %fusion = f32[64,1024]{1,0:T(8,128)} fusion(f32[64,512]{1,0:T(8,128)} %shard_map.42, f32[512,1024]{1,0:T(8,128)S(1)} %bitcast.16), kind=kOutput, calls=%fused_computation.9 | convolution fusion | flops 201326592 | bytes 2490368 | tf_op jit(solution)/shard_map/dot_general | solution.py:149
  (9 shorter events, 0.3 us)
Async XLA Ops:
  3.8 16.9 %copy-start = (f32[512,64]{0,1:T(8,128)S(1)}, f32[512,64]{0,1:T(8,128)}, u32[]{:S(2)}) copy-start(f32[512,64]{0,1:T(8,128)} %param.3) | copy-start | bytes 393220
  3.8 115.5 %all-to-all-start = ((f32[16,32,1024]{2,0,1:T(8,128)}), f32[16,32,1024]{2,0,1:T(8,128)S(1)}, u32[]{:S(2)}, u32[]{:S(2)}) async-start(f32[16,32,1024]{2,0,1:T(8,128)} %bitcast.17), calls=%async_computation | async-start | bytes 4194304 | tf_op jit(solution)/shard_map/all_to_all | solution.py:143
